TPU v7x, 32 devices: a whole 2x2x4 slice. The times are simulated.
32 devices in a mesh: gx: 4 (over y, x), gy: 8 (over z, core).
Axes of the slice: x: 2, y: 2, z: 4, core: 2. Of those that a mesh axis runs over, the one named last changes fastest.
Arguments:
- atom_data: float32 [4, 16, 32, 2, 128], P(None, 'gx', 'gy'), as said below
- counts: int32 [16, 32, 2], P('gx', 'gy'), may hold values from 32 to 128, as said below
- near_flags: int32 [26, 16, 32, 2], P(None, 'gx', 'gy'), may hold values 0 or 1
- child_up: bfloat16 [8, 81, 81], replicated, may hold values from -0.25 to 0.25
- child_down: bfloat16 [8, 81, 81], replicated, may hold values from -0.5 to 0.5
- leaf_far: bfloat16 [81, 81], replicated, may hold values from -0.1875 to 0.1875
- parent_far: bfloat16 [81, 81], replicated, may hold values from -0.0625 to 0.0625
- column_up: bfloat16 [81, 81], replicated, may hold values from -0.3125 to 0.3125
- column_down: bfloat16 [81, 81], replicated, may hold values from -0.5 to 0.5
- tree_up: bfloat16 [2, 2, 81, 81], replicated, may hold values from -0.5 to 0.5
- tree_down: bfloat16 [2, 2, 81, 81], replicated, may hold values from -0.5 to 0.5
- tree_side: bfloat16 [2, 2, 81, 81], replicated, may hold values from -0.5 to 0.5
- lattice: bfloat16 [81, 81], replicated, may hold values from -0.625 to 0.625
Outputs:
- fields: float32 [4, 16, 32, 2, 128], P(None, 'gx', 'gy')
Inputs may be any that keep to these rules, and one draw needn't show every extreme that they name: `atom_data`: rows 0 to 2 give an atom's position inside its leaf in leaf widths, from 0 to 1; row 3 its charge. Slots at or past a leaf's count are padding. A leaf's atoms fill its first counts slots; some leaf is full.
All inputs are finite; a program needn't handle non-finite values. No bound on the sum of `near_flags` on one device may be relied on, other than what follows from the above.
Results may differ from a plain program's by a relative error of at most 0.0003.
Values sent between devices are 32-bit elements; how exact they have to be, the bound alone decides.
No kernel may reach another device: no remote copies, remote signals or barrier semaphores. Data moves between devices by JAX's collectives and lax.ppermute only.
A program may use at most 64 MiB of HBM per device.

v0:
```python
import functools

import jax
import jax.numpy as jnp
from jax import lax
from jax.experimental import pallas as pl
from jax.experimental.pallas import tpu as pltpu
from jax.sharding import PartitionSpec as P

soften = 0.04
coulomb = 0.1
highest = lax.Precision.HIGHEST


def from_partner(value, axis, bit):
    mask = 2**bit
    pairs = [(source, source ^ mask) for source in range(lax.axis_size(axis))]
    return lax.ppermute(value, axis, pairs)


def extended_2(block, sides, width):
    return extended_joint([(block, width)], sides)[0]


def extended_joint(parts, sides):
    blocks = [block for block, width in parts]
    for axis, dim in sides:
        count = lax.axis_size(axis)
        forward = [(i, i + 1) for i in range(count - 1)]
        forward.append((count - 1, 0))
        backward = [(target, source) for source, target in forward]
        lows = [lax.slice_in_dim(b, b.shape[dim] - w, None, axis=dim) for b, (_, w) in zip(blocks, parts)]
        highs = [lax.slice_in_dim(b, 0, w, axis=dim) for b, (_, w) in zip(blocks, parts)]
        sizes = [piece.size for piece in lows]
        low_all = lax.ppermute(jnp.concatenate([piece.reshape(-1) for piece in lows]), axis, forward)
        high_all = lax.ppermute(jnp.concatenate([piece.reshape(-1) for piece in highs]), axis, backward)
        grown = []
        place = 0
        for b, piece, size in zip(blocks, lows, sizes):
            low = low_all[place : place + size].reshape(piece.shape)
            high = high_all[place : place + size].reshape(piece.shape)
            place += size
            grown.append(jnp.concatenate([low, b, high], axis=dim))
        blocks = grown
    return blocks


def wave_table(coef_count, float_type):
    half_count = (coef_count - 1) // 2
    order_index = jnp.arange(1, half_count + 1, dtype=jnp.int32).astype(float_type)
    height = 1.0 - 2.0 * (order_index - 0.5) / half_count
    radius = jnp.sqrt(jnp.maximum(1.0 - height * height, 0.0))
    angle_turn = 2.399963 * order_index
    magnitude = 1.5 + jnp.mod(order_index, 3.0)
    return (
        jnp.stack([radius * jnp.cos(angle_turn), radius * jnp.sin(angle_turn), height])
        * magnitude[None]
    )


def waves_at(atom_data, waves):
    shape_lead = (waves.shape[1],) + (1,) * (atom_data.ndim - 1)
    phases = waves[0].reshape(shape_lead) * (atom_data[0] - 0.5)[None]
    phases = phases + waves[1].reshape(shape_lead) * (atom_data[1] - 0.5)[None]
    phases = phases + waves[2].reshape(shape_lead) * (atom_data[2] - 0.5)[None]
    return (jnp.cos(phases), jnp.sin(phases))


def rotate_by(field, phase):
    half_count = phase.shape[0]
    cosine = jnp.cos(phase)
    sine_part = jnp.sin(phase)
    cos_coef = field[1 : 1 + half_count]
    sin_coef = field[1 + half_count :]
    return jnp.concatenate(
        [
            field[0:1],
            cos_coef * cosine - sin_coef * sine_part,
            cos_coef * sine_part + sin_coef * cosine,
        ],
        axis=0,
    )


def offset_phases(waves, offsets):
    table = jnp.array(offsets, dtype=jnp.float32)
    return (
        table[:, 0:1] * waves[0][None]
        + table[:, 1:2] * waves[1][None]
        + table[:, 2:3] * waves[2][None]
    )


def block_phase(waves, size_x, size_y, size_z, float_type):
    place_x = jnp.arange(size_x, dtype=jnp.int32).astype(float_type)
    place_y = jnp.arange(size_y, dtype=jnp.int32).astype(float_type)
    place_z = jnp.arange(size_z, dtype=jnp.int32).astype(float_type)
    phase = waves[0][:, None, None, None] * place_x[None, :, None, None]
    phase = phase + waves[1][:, None, None, None] * place_y[None, None, :, None]
    return phase + waves[2][:, None, None, None] * place_z[None, None, None, :]


def leaf_moments(atom_data, waves):
    cosine, sine_part = waves_at(atom_data, waves)
    charge = atom_data[3]
    summed = jnp.sum(charge, axis=-1)[None]
    return jnp.concatenate(
        [
            summed,
            jnp.sum(cosine * charge[None], axis=-1),
            jnp.sum(sine_part * charge[None], axis=-1),
        ],
        axis=0,
    )


def evaluate(atom_data, local_exp, waves):
    cosine, sine_part = waves_at(atom_data, waves)
    half_count = waves.shape[1]
    cos_local = local_exp[1 : 1 + half_count][..., None]
    sin_local = local_exp[1 + half_count :][..., None]
    potential = local_exp[0][..., None] + jnp.sum(
        cos_local * cosine + sin_local * sine_part, axis=0
    )
    mixed_term = cos_local * sine_part - sin_local * cosine
    shape_lead = (half_count,) + (1,) * (mixed_term.ndim - 1)
    field_parts = [
        jnp.sum(waves[component].reshape(shape_lead) * mixed_term, axis=0) for component in range(3)
    ]
    return (potential, field_parts)


def near_row(target, source, flag_grid, shift_vec, keep_self):
    weight = source[3] * flag_grid[..., None]
    delta_x = target[0][..., :, None] - (source[0][..., None, :] + shift_vec[0])
    delta_y = target[1][..., :, None] - (source[1][..., None, :] + shift_vec[1])
    delta_z = target[2][..., :, None] - (source[2][..., None, :] + shift_vec[2])
    inverse = lax.rsqrt(delta_x * delta_x + delta_y * delta_y + delta_z * delta_z + soften)
    pair_term = weight[..., None, :] * keep_self * inverse
    cube_term = pair_term * inverse * inverse
    return jnp.stack(
        [
            jnp.sum(pair_term, axis=-1),
            jnp.sum(cube_term * delta_x, axis=-1),
            jnp.sum(cube_term * delta_y, axis=-1),
            jnp.sum(cube_term * delta_z, axis=-1),
        ]
    )


def full_flags(near_flags, float_type):
    flags_float = near_flags.astype(float_type)
    centre = jnp.ones((1,) + flags_float.shape[1:], float_type)
    return jnp.concatenate([flags_float[:13], centre, flags_float[13:]], axis=0)


def leaf_offsets():
    return [
        (shift_x, shift_y, shift_z)
        for shift_x in (-1, 0, 1)
        for shift_y in (-1, 0, 1)
        for shift_z in (-1, 0, 1)
        if (shift_x, shift_y, shift_z) != (0, 0, 0)
    ]


def parent_offsets():
    return [
        (shift_x, shift_y, shift_z)
        for shift_x in range(-2, 3)
        for shift_y in range(-2, 3)
        for shift_z in range(-2, 3)
        if max(abs(shift_x), abs(shift_y), abs(shift_z)) == 2
    ]


def climb_children(moments, matrices):
    coef_count, size_x, size_y, size_z = moments.shape
    parted = moments.reshape(coef_count, size_x // 2, 2, size_y // 2, 2, size_z // 2, 2)
    return jnp.einsum(
        "abckj,jxaybzc->kxyz",
        matrices.reshape(2, 2, 2, coef_count, coef_count),
        parted,
        precision=highest,
    )


def descend_children(parent_local, matrices):
    coef_count, size_x, size_y, size_z = parent_local.shape
    spread = jnp.einsum(
        "abckj,jxyz->kxaybzc",
        matrices.reshape(2, 2, 2, coef_count, coef_count),
        parent_local,
        precision=highest,
    )
    return spread.reshape(coef_count, 2 * size_x, 2 * size_y, 2 * size_z)


def matrix_vector(matrix, vector):
    return jnp.dot(matrix, vector, precision=highest)


def pick_side(matrices, own_side):
    return lax.dynamic_index_in_dim(matrices, own_side, 0, keepdims=False)


def pair_step(matrices, own_side, current, partner):
    return matrix_vector(pick_side(matrices, own_side), current) + matrix_vector(
        pick_side(matrices, 1 - own_side), partner
    )


def chain_tree(column, tree_up, tree_down, tree_side, lattice, hook):
    climbs = tree_up.astype(jnp.float32)
    lowers = tree_down.astype(jnp.float32)
    sideways = tree_side.astype(jnp.float32)
    current = column
    visited = []
    partner = None
    for level_bit in range(lax.axis_size("gx").bit_length() - 1):
        current = hook(current, partner)
        partner = from_partner(current, "gx", level_bit)
        own_side = lax.axis_index("gx") // 2**level_bit % 2
        current = pair_step(climbs[0], own_side, current, partner)
        visited.append((0, own_side, partner))
    for level_bit in range(lax.axis_size("gy").bit_length() - 1):
        current = hook(current, partner)
        partner = from_partner(current, "gy", level_bit)
        own_side = lax.axis_index("gy") // 2**level_bit % 2
        current = pair_step(climbs[1], own_side, current, partner)
        visited.append((1, own_side, partner))
    local_exp = matrix_vector(lattice.astype(jnp.float32), current)
    for axis_num, own_side, partner in reversed(visited):
        local_exp = matrix_vector(pick_side(lowers[axis_num], own_side), local_exp) + matrix_vector(
            pick_side(sideways[axis_num], own_side), partner
        )
    return local_exp


def flip_pair(column_grid, axis_num, level_bit):
    coef_count, size_x, size_y = column_grid.shape
    span_size = 2**level_bit
    if axis_num == 0:
        parted = column_grid.reshape(coef_count, size_x // (2 * span_size), 2, span_size, size_y)
        return parted[:, :, ::-1].reshape(column_grid.shape)
    parted = column_grid.reshape(coef_count, size_x, size_y // (2 * span_size), 2, span_size)
    return parted[:, :, :, ::-1].reshape(column_grid.shape)


def side_grid(axis_num, level_bit, size_x, size_y):
    positions = jnp.arange(size_x if axis_num == 0 else size_y, dtype=jnp.int32)
    own_side = positions // 2**level_bit % 2
    return own_side[:, None] if axis_num == 0 else own_side[None, :]


def choose_side(matrices, own_side, column_grid):
    first = jnp.einsum("kj,jxy->kxy", matrices[0], column_grid, precision=highest)
    second = jnp.einsum("kj,jxy->kxy", matrices[1], column_grid, precision=highest)
    return jnp.where(own_side[None] == 0, first, second)


def gathered_tree(column, tree_up, tree_down, tree_side, lattice):
    size_x, size_y = lax.axis_size("gx"), lax.axis_size("gy")
    gathered = lax.all_gather(column, ("gx", "gy")).reshape(size_x, size_y, -1)
    current = jnp.transpose(gathered, (2, 0, 1))
    levels = [(0, bit) for bit in range(size_x.bit_length() - 1)] + [
        (1, bit) for bit in range(size_y.bit_length() - 1)
    ]
    visited = []
    for axis_num, level_bit in levels:
        partner = flip_pair(current, axis_num, level_bit)
        own_side = side_grid(axis_num, level_bit, size_x, size_y)
        climbs = tree_up[axis_num].astype(jnp.float32)
        current = choose_side(climbs, own_side, current) + choose_side(climbs, 1 - own_side, partner)
        visited.append((axis_num, own_side, partner))
    local_exp = jnp.einsum("kj,jxy->kxy", lattice.astype(jnp.float32), current, precision=highest)
    for axis_num, own_side, partner in reversed(visited):
        local_exp = choose_side(tree_down[axis_num].astype(jnp.float32), own_side, local_exp) + choose_side(
            tree_side[axis_num].astype(jnp.float32), own_side, partner
        )
    own = lax.dynamic_slice(local_exp, (0, lax.axis_index("gx"), lax.axis_index("gy")), (local_exp.shape[0], 1, 1))
    return own.reshape(-1)


def assemble(near_terms, potential, field_parts, charge, live_slots):
    rows = [coulomb * (near_terms[0] + potential) * live_slots]
    for component in range(3):
        rows.append(coulomb * charge * (near_terms[1 + component] + field_parts[component]))
    return jnp.stack(rows)


NEAR_ROWS = 64
NEAR_PIECES = 8
NEAR_UNROLL = 2


def near_pairs(tx, ty, tz, srow, mask):
    weight = srow[3:4, :]
    delta_x = tx - srow[0:1, :]
    delta_y = ty - srow[1:2, :]
    delta_z = tz - srow[2:3, :]
    inverse = lax.rsqrt(delta_x * delta_x + delta_y * delta_y + delta_z * delta_z + soften)
    pair_term = weight * inverse
    if mask is not None:
        pair_term = jnp.where(mask, pair_term, 0.0)
    cube_term = pair_term * inverse * inverse
    return (pair_term, cube_term * delta_x, cube_term * delta_y, cube_term * delta_z)


def near_kernel(first_leaf, leaf_count, listed_width, table_ref, target_ref, source_ref, shift_ref, out_ref, tile_ref):
    piece_leaves = out_ref.shape[0]
    place_start = 2 * leaf_count
    kind_start = place_start + leaf_count * listed_width
    big = NEAR_ROWS
    small = NEAR_ROWS // 2
    lanes = out_ref.shape[2]

    def leaf_body(local, carry):
        leaf = first_leaf + local
        count = table_ref[leaf]
        full_count = count // big
        rest = count - full_count * big
        listed = table_ref[leaf_count + leaf]
        base = leaf * listed_width
        tile_ref[...] = jnp.zeros(tile_ref.shape, tile_ref.dtype)

        def chunk_at(first, rows):
            lane = lax.broadcasted_iota(jnp.int32, (rows, lanes), 1)
            row = lax.broadcasted_iota(jnp.int32, (rows, lanes), 0)
            column = target_ref[local, pl.ds(first, rows), :]
            tx = jnp.broadcast_to(column[:, 0:1], (rows, lanes))
            ty = jnp.broadcast_to(column[:, 1:2], (rows, lanes))
            tz = jnp.broadcast_to(column[:, 2:3], (rows, lanes))
            acc = near_pairs(tx, ty, tz, source_ref[table_ref[place_start + base]], row + first != lane)

            def offset_body(step, acc):
                number = base + 1 + NEAR_UNROLL * step
                for extra in range(NEAR_UNROLL):
                    srow = source_ref[table_ref[place_start + number + extra]]
                    srow = srow + shift_ref[table_ref[kind_start + number + extra]]
                    terms = near_pairs(tx, ty, tz, srow, None)
                    acc = tuple(a + b for a, b in zip(acc, terms))
                return acc

            acc = lax.fori_loop(0, (listed - 1) // NEAR_UNROLL, offset_body, acc)
            sums = [jnp.sum(part, axis=1, keepdims=True) for part in acc]
            tile = jnp.where(
                lane == 0, sums[0], jnp.where(lane == 1, sums[1], jnp.where(lane == 2, sums[2], sums[3]))
            )
            tile_ref[pl.ds(first, rows), :] = jnp.where(lane < 4, tile, 0.0)

        def full_body(chunk, carry2):
            chunk_at(pl.multiple_of(chunk * big, big), big)
            return carry2

        lax.fori_loop(0, full_count, full_body, 0)
        last = pl.multiple_of(full_count * big, small)

        @pl.when(rest > small)
        def _():
            chunk_at(last, big)

        @pl.when((rest > 0) & (rest <= small))
        def _():
            chunk_at(last, small)

        out_ref[local] = jnp.transpose(tile_ref[...])[0 : out_ref.shape[1], :]
        return carry

    lax.fori_loop(0, piece_leaves, leaf_body, 0)


def near_local(charged, rimmed, counts, near_flags):
    size_x, size_y, size_z, slot_count = charged.shape[1:]
    leaf_count = size_x * size_y * size_z
    ext_y = size_y + 2
    target = jnp.transpose(charged, (1, 2, 3, 4, 0)).reshape(leaf_count, slot_count, 4)
    source = jnp.transpose(rimmed, (1, 2, 3, 0, 4)).reshape(-1, 4, slot_count)
    source = jnp.pad(source, ((0, 1), (0, 4), (0, 0)))
    empty_leaf = source.shape[0] - 1
    offsets = [(0, 0, 0)] + leaf_offsets()
    shift_rows = jnp.array([[float(v) for v in offset] + [0.0] * 5 for offset in offsets], jnp.float32)
    shift_table = jnp.broadcast_to(shift_rows[:, :, None], (len(offsets), 8, slot_count))
    leaf_x = jnp.arange(size_x, dtype=jnp.int32)[:, None, None]
    leaf_y = jnp.arange(size_y, dtype=jnp.int32)[None, :, None]
    leaf_z = jnp.arange(size_z, dtype=jnp.int32)[None, None, :]
    places = []
    for offset in offsets:
        place = ((leaf_x + 1 + offset[0]) * ext_y + leaf_y + 1 + offset[1]) * size_z + leaf_z + offset[2]
        places.append(jnp.broadcast_to(place, (size_x, size_y, size_z)))
    places = jnp.stack(places).reshape(len(offsets), leaf_count)
    layer = jnp.arange(size_z, dtype=jnp.int32)
    valid = jnp.stack([((layer + offset[2] >= 0) & (layer + offset[2] < size_z)) for offset in offsets[1:]])
    active = (near_flags != 0) & valid[:, None, None, :]
    active = jnp.concatenate([jnp.ones((1, leaf_count), bool), active.reshape(len(offsets) - 1, leaf_count)])
    listed = jnp.sum(active.astype(jnp.int32), axis=0)
    listed = listed + (NEAR_UNROLL - (listed - 1) % NEAR_UNROLL) % NEAR_UNROLL
    position = jnp.cumsum(active.astype(jnp.int32), axis=0) - 1
    width = 1 + -(-(len(offsets) - 1) // NEAR_UNROLL) * NEAR_UNROLL
    slots = jnp.arange(width, dtype=jnp.int32)
    chosen = active[None] & (position[None] == slots[:, None, None])
    kinds = jnp.arange(len(offsets), dtype=jnp.int32)
    kind_list = jnp.sum(jnp.where(chosen, kinds[None, :, None], 0), axis=1)
    place_list = jnp.sum(jnp.where(chosen, places[None], 0), axis=1)
    place_list = jnp.where(slots[:, None] < jnp.sum(active.astype(jnp.int32), axis=0)[None], place_list, empty_leaf)
    table = jnp.concatenate(
        [counts.reshape(-1), listed, jnp.transpose(place_list).reshape(-1), jnp.transpose(kind_list).reshape(-1)]
    ).astype(jnp.int32)
    piece = leaf_count // NEAR_PIECES if leaf_count % NEAR_PIECES == 0 else leaf_count
    pairs = piece * slot_count * slot_count * 10

    def run_piece(number, gate):
        first_leaf = number * piece
        own = target[first_leaf : first_leaf + piece]
        if gate is not None:
            own, unused = lax.optimization_barrier((own, gate))
        return pl.pallas_call(
            functools.partial(near_kernel, first_leaf, leaf_count, width),
            out_shape=jax.ShapeDtypeStruct((piece, 8, slot_count), jnp.float32),
            in_specs=[pl.BlockSpec(memory_space=pltpu.SMEM)] + [pl.BlockSpec(memory_space=pltpu.VMEM)] * 3,
            out_specs=pl.BlockSpec(memory_space=pltpu.VMEM),
            scratch_shapes=[pltpu.VMEM((slot_count, 128), jnp.float32)],
            cost_estimate=pl.CostEstimate(
                flops=20 * pairs, transcendentals=pairs, bytes_accessed=8 * piece * slot_count * 128
            ),
        )(table, own, source, shift_table)

    def finish_near(outs):
        out = jnp.concatenate(outs, axis=0)
        near = jnp.transpose(out[:, :4, :], (1, 0, 2))
        return near.reshape(4, size_x, size_y, size_z, slot_count)

    return leaf_count // piece, run_piece, finish_near


def body(
    atom_data,
    counts,
    near_flags,
    child_up,
    child_down,
    leaf_far,
    parent_far,
    column_up,
    column_down,
    tree_up,
    tree_down,
    tree_side,
    lattice,
):
    coef_count = lattice.shape[0]
    slot_count = atom_data.shape[4]
    size_x, size_y, size_z = (atom_data.shape[1], atom_data.shape[2], atom_data.shape[3])
    live_slots = (
        jnp.arange(slot_count, dtype=jnp.int32)[None, None, None, :] < counts[..., None]
    ).astype(jnp.float32)
    charged = jnp.concatenate([atom_data[:3], (atom_data[3] * live_slots)[None]], axis=0)
    waves = wave_table(coef_count, jnp.float32)
    half_count = waves.shape[1]
    moments = leaf_moments(charged, waves)
    parents = climb_children(moments, child_up.astype(jnp.float32))
    rimmed, parent_rim, leaf_rim = extended_joint([(charged, 1), (parents, 2), (moments, 1)], (("gx", 1), ("gy", 2)))
    parent_rim = jnp.pad(parent_rim, ((0, 0), (0, 0), (0, 0), (2, 2)))
    half_x, half_y, half_z = (parents.shape[1], parents.shape[2], parents.shape[3])
    phase_grid = block_phase(waves, half_x, half_y, half_z, jnp.float32)
    turned = jnp.sum(rotate_by(parents, phase_grid), axis=(1, 2, 3))
    column = matrix_vector(column_up.astype(jnp.float32), turned)
    piece_count, run_piece, finish_near = near_local(charged, rimmed, counts, near_flags)
    pieces = []

    def hook(value, prior):
        number = len(pieces)
        if number < piece_count:
            if number > 0:
                value, unused = lax.optimization_barrier((value, pieces[-1]))
            pieces.append(run_piece(number, prior))
        return value

    column_local = chain_tree(column, tree_up, tree_down, tree_side, lattice, hook)
    while len(pieces) < piece_count:
        pieces.append(run_piece(len(pieces), None))
    near_terms = finish_near(pieces)
    leaf_rim = jnp.pad(leaf_rim, ((0, 0), (0, 0), (0, 0), (1, 1)))
    lowered = matrix_vector(column_down.astype(jnp.float32), column_local)
    parent_local = rotate_by(
        jnp.broadcast_to(lowered[:, None, None, None], parents.shape), -phase_grid
    )
    far_parents = parent_offsets()
    parent_stack = jnp.stack(
        [
            parent_rim[
                :,
                2 + offset[0] : 2 + offset[0] + half_x,
                2 + offset[1] : 2 + offset[1] + half_y,
                2 + offset[2] : 2 + offset[2] + half_z,
            ]
            for offset in far_parents
        ]
    )
    parent_turns = offset_phases(waves, far_parents).reshape(len(far_parents), half_count, 1, 1, 1)
    parent_sum = jnp.sum(jax.vmap(rotate_by)(parent_stack, parent_turns), axis=0)
    parent_local = parent_local + jnp.einsum(
        "kj,jxyz->kxyz", parent_far.astype(jnp.float32), parent_sum, precision=highest
    )
    leaf_local = descend_children(parent_local, child_down.astype(jnp.float32))
    near_leaves = leaf_offsets()
    leaf_stack = jnp.stack(
        [
            leaf_rim[
                :,
                1 + offset[0] : 1 + offset[0] + size_x,
                1 + offset[1] : 1 + offset[1] + size_y,
                1 + offset[2] : 1 + offset[2] + size_z,
            ]
            for offset in near_leaves
        ]
    )
    leaf_stack = leaf_stack * (1.0 - near_flags.astype(jnp.float32))[:, None]
    leaf_turns = offset_phases(waves, near_leaves).reshape(len(near_leaves), half_count, 1, 1, 1)
    leaf_sum = jnp.sum(jax.vmap(rotate_by)(leaf_stack, leaf_turns), axis=0)
    leaf_local = leaf_local + jnp.einsum(
        "kj,jxyz->kxyz", leaf_far.astype(jnp.float32), leaf_sum, precision=highest
    )
    potential, field_parts = evaluate(charged, leaf_local, waves)
    return assemble(near_terms, potential, field_parts, charged[3], live_slots)


def solution(mesh):
    in_specs = (
        P(None, "gx", "gy", None, None),
        P("gx", "gy", None),
        P(None, "gx", "gy", None),
        P(),
        P(),
        P(),
        P(),
        P(),
        P(),
        P(),
        P(),
        P(),
        P(),
    )
    out_specs = P(None, "gx", "gy", None, None)
    return jax.shard_map(body, mesh=mesh, in_specs=in_specs, out_specs=out_specs, check_vma=False)
```

profile of v0, /device:TPU:0, one launch (start us, length us, event | category | flops | bytes accessed | tf_op | source)
XLA Modules:
  0.0 103.7 jit_solution(499316776183701192)
XLA Ops:
  0.1 0.8 copy.357
  0.9 0.8 slice.563
  1.7 0.9 add_bitcast_fusion.2
  2.6 0.9 fusion.42
  3.5 2.9 %multiply_reduce_fusion.4 = (f32[40,4,4,2]{0,3,2,1:T(2,128)S(1)}, f32[40,4,4,2]{0,3,2,1:T(2,128)S(1)}) fusion(f32[4,4,2,128]{3,2,1,0:T(2,128)S(1)} %bitcast.458, f32[4,4,2,128]{3,2,1,0:T(2,128)S(1)} %get-tuple-element.75, f32[40]{0:T(128)S(1)} %get-tuple-element.130, f32[4,4,2,128]{3,2,1,0:T(2,128)S(1)} %get-tuple-element.76, f32[40]{0:T(128)S(1)} %get-tuple-element.131, ...), kind=kLoop, calls=%fused_computation.50 | loop fusion | flops 1472000 | bytes 76256 | tf_op jit(solution)/shard_map/reduce_sum | solution.py:110
  8.1 3.9 %collective-permute-start.1 = (f32[5068]{0:T(1024)S(1)}, f32[5068]{0:T(1024)S(1)}, u32[]{:S(2)}, u32[]{:S(2)}) collective-permute-start(f32[5068]{0:T(1024)S(1)} %concatenate.99), channel_id=1, source_target_pairs={{8,0},{16,8},{24,16},{0,24},{9,1},{17,9},{25,17},{1,25},{10,2},{18... | collective-permute-start | bytes 60824 | tf_op jit(solution)/shard_map/ppermute | solution.py:36
  12.8 2.0 %collective-permute-start.4 = (f32[81]{0:T(128)S(1)}, f32[81]{0:T(128)S(1)}, u32[]{:S(2)}, u32[]{:S(2)}) collective-permute-start(f32[81]{0:T(128)S(1)} %bitcast.493), channel_id=1, source_target_pairs={{0,8},{8,0},{16,24},{24,16},{1,9},{9,1},{17,25},{25,17},{2,10},{10... | collective-permute-start | bytes 980 | tf_op jit(solution)/shard_map/ppermute | solution.py:18
  17.4 0.6 copy.362
  18.1 1.3 %fusion.94 = (f32[4,128,4]{2,1,0:T(8,128)}, f32[4,128,4]{2,1,0:T(8,128)}, f32[4,128,4]{2,1,0:T(8,128)}, f32[4,128,4]{2,1,0:T(8,128)}, f32[4,128,4]{2,1,0:T(8,128...) fusion(f32[32,128,4]{2,1,0:T(8,128)S(1)} %bitcast.455), kind=kLoop, calls=%fused_computation.470 | loop fusion | bytes 131072 | tf_op jit(solution)/shard_map/slice | solution.py:414
  22.1 0.7 concatenate.91.table_ref
  25.2 2.2 %collective-permute-start.3 = (f32[8088]{0:T(1024)S(1)}, f32[8088]{0:T(1024)S(1)}, u32[]{:S(2)}, u32[]{:S(2)}) collective-permute-start(f32[8088]{0:T(1024)S(1)} %concatenate.104), channel_id=1, source_target_pairs={{1,0},{2,1},{3,2},{4,3},{5,4},{6,5},{7,6},{0,7},{9,8},{10,9},{11,1... | collective-permute-start | bytes 97064 | tf_op jit(solution)/shard_map/ppermute | solution.py:36
  29.6 4.2 %collective-permute-done.2 = f32[8088]{0:T(1024)S(1)} collective-permute-done((f32[8088]{0:T(1024)S(1)}, f32[8088]{0:T(1024)S(1)}, u32[]{:S(2)}, u32[]{:S(2)}) %collective-permute-start.2) | collective-permute-done | bytes 32384 | tf_op jit(solution)/shard_map/ppermute | solution.py:35
  34.3 0.7 pad.11.source_ref
  35.1 0.7 broadcast_in_dim.44.shift_ref
  35.8 4.4 %shard_map.154 = f32[4,8,128]{2,1,0:T(8,128)} custom-call(s32[1792]{0:T(1024)} %concatenate.91.table_ref, f32[4,128,4]{2,1,0:T(8,128)} %get-tuple-element.36.target_ref, f32[73,8,128]{2,1,0:T(8,128)} %pad.11.source_ref, f32[27,8,128]{2,1,0:T(8,128)} %broadcast_in_dim.44.shift_ref), custom_call_target="tpu_custom_call" | custom-call | flops 13107200 | bytes 524288 | tf_op jit(solution)/shard_map/pallas_call | solution.py:417
  40.2 0.7 constant_dynamic-update-slice_fusion.7
  40.9 5.2 %shard_map.155 = f32[4,8,128]{2,1,0:T(8,128)} custom-call(s32[1792]{0:T(1024)} %concatenate.91.table_ref, f32[4,128,4]{2,1,0:T(8,128)} %get-tuple-element.13.target_ref, f32[73,8,128]{2,1,0:T(8,128)} %pad.11.source_ref, f32[27,8,128]{2,1,0:T(8,128)} %broadcast_in_dim.44.shift_ref), custom_call_target="tpu_custom_call" | custom-call | flops 13107200 | bytes 524288 | tf_op jit(solution)/shard_map/pallas_call | solution.py:417
  46.1 2.9 %collective-permute-start.5 = (f32[81]{0:T(128)S(1)}, f32[81]{0:T(128)S(1)}, u32[]{:S(2)}, u32[]{:S(2)}) collective-permute-start(f32[81]{0:T(128)S(1)} %fusion.12), channel_id=1, source_target_pairs={{0,16},{8,24},{16,0},{24,8},{1,17},{9,25},{17,1},{25,9},{2,18},{10... | collective-permute-start | bytes 980 | tf_op jit(solution)/shard_map/ppermute | solution.py:18
  49.1 6.2 %shard_map.159 = f32[4,8,128]{2,1,0:T(8,128)} custom-call(s32[1792]{0:T(1024)} %concatenate.91.table_ref, f32[4,128,4]{2,1,0:T(8,128)} %get-tuple-element.31.target_ref, f32[73,8,128]{2,1,0:T(8,128)} %pad.11.source_ref, f32[27,8,128]{2,1,0:T(8,128)} %broadcast_in_dim.44.shift_ref), custom_call_target="tpu_custom_call" | custom-call | flops 13107200 | bytes 524288 | tf_op jit(solution)/shard_map/pallas_call | solution.py:417
  55.3 5.0 %shard_map.160 = f32[4,8,128]{2,1,0:T(8,128)} custom-call(s32[1792]{0:T(1024)} %concatenate.91.table_ref, f32[4,128,4]{2,1,0:T(8,128)} %get-tuple-element.30.target_ref, f32[73,8,128]{2,1,0:T(8,128)} %pad.11.source_ref, f32[27,8,128]{2,1,0:T(8,128)} %broadcast_in_dim.44.shift_ref), custom_call_target="tpu_custom_call" | custom-call | flops 13107200 | bytes 524288 | tf_op jit(solution)/shard_map/pallas_call | solution.py:417
  63.5 0.5 maximum_reduce_fusion
  65.0 6.2 %shard_map.161 = f32[4,8,128]{2,1,0:T(8,128)} custom-call(s32[1792]{0:T(1024)} %concatenate.91.table_ref, f32[4,128,4]{2,1,0:T(8,128)} %get-tuple-element.29.target_ref, f32[73,8,128]{2,1,0:T(8,128)} %pad.11.source_ref, f32[27,8,128]{2,1,0:T(8,128)} %broadcast_in_dim.44.shift_ref), custom_call_target="tpu_custom_call" | custom-call | flops 13107200 | bytes 524288 | tf_op jit(solution)/shard_map/pallas_call | solution.py:417
  71.3 4.9 %shard_map.156 = f32[4,8,128]{2,1,0:T(8,128)} custom-call(s32[1792]{0:T(1024)} %concatenate.91.table_ref, f32[4,128,4]{2,1,0:T(8,128)} %get-tuple-element.15.target_ref, f32[73,8,128]{2,1,0:T(8,128)} %pad.11.source_ref, f32[27,8,128]{2,1,0:T(8,128)} %broadcast_in_dim.44.shift_ref), custom_call_target="tpu_custom_call" | custom-call | flops 13107200 | bytes 524288 | tf_op jit(solution)/shard_map/pallas_call | solution.py:417
  76.4 0.8 constant_dynamic-update-slice_fusion.5
  77.5 4.8 %shard_map.157 = f32[4,8,128]{2,1,0:T(8,128)} custom-call(s32[1792]{0:T(1024)} %concatenate.91.table_ref, f32[4,128,4]{2,1,0:T(8,128)} %get-tuple-element.17.target_ref, f32[73,8,128]{2,1,0:T(8,128)} %pad.11.source_ref, f32[27,8,128]{2,1,0:T(8,128)} %broadcast_in_dim.44.shift_ref), custom_call_target="tpu_custom_call" | custom-call | flops 13107200 | bytes 524288 | tf_op jit(solution)/shard_map/pallas_call | solution.py:417
  82.5 0.8 constant_dynamic-update-slice_fusion.4
  83.3 2.7 %collective-permute-done.7 = f32[81]{0:T(128)S(1)} collective-permute-done((f32[81]{0:T(128)S(1)}, f32[81]{0:T(128)S(1)}, u32[]{:S(2)}, u32[]{:S(2)}) %collective-permute-start.7) | collective-permute-done | bytes 356 | tf_op jit(solution)/shard_map/ppermute | solution.py:18
  86.0 5.0 %shard_map.158 = f32[4,8,128]{2,1,0:T(8,128)} custom-call(s32[1792]{0:T(1024)} %concatenate.91.table_ref, f32[4,128,4]{2,1,0:T(8,128)} %get-tuple-element.19.target_ref, f32[73,8,128]{2,1,0:T(8,128)} %pad.11.source_ref, f32[27,8,128]{2,1,0:T(8,128)} %broadcast_in_dim.44.shift_ref), custom_call_target="tpu_custom_call" | custom-call | flops 13107200 | bytes 524288 | tf_op jit(solution)/shard_map/pallas_call | solution.py:417
  91.0 0.7 constant_dynamic-update-slice_fusion.3
  92.1 4.3 %collective-permute-done.8 = f32[81]{0:T(128)S(1)} collective-permute-done((f32[81]{0:T(128)S(1)}, f32[81]{0:T(128)S(1)}, u32[]{:S(2)}, u32[]{:S(2)}) %collective-permute-start.8) | collective-permute-done | bytes 356 | tf_op jit(solution)/shard_map/ppermute | solution.py:18
  100.0 3.0 %add_reduce_fusion = (f32[4,4,2,128]{3,2,1,0:T(2,128)S(1)}, f32[4,4,2,128]{3,2,1,0:T(2,128)S(1)}, f32[4,4,2,128]{3,2,1,0:T(2,128)S(1)}, f32[4,4,2,128]{3,2,1,0:T(2,128)S(1)}) fusion(f32[40,4,4,2]{0,3,2,1:T(2,128)S(1)} %copy.449, f32[40,4,4,2]{0,3,2,1:T(2,128)S(1)} %copy.448, f32[4,4,2,128]{3,2,1,0:T(2,128)S(1)} %get-tuple-element.75, ...), kind=kLoop, calls=%fused_computation.48 | loop fusion | flops 2932736 | bytes 125408 | tf_op jit(solution)/shard_map/reduce_sum | solution.py:122
  103.1 0.7 pad_maximum_fusion.1
  (365 shorter events, 20.8 us)
Async XLA Ops:
  0.0 6.7 %copy-start = (bf16[8,81,81]{2,0,1:T(8,128)(2,1)S(1)}, bf16[8,81,81]{2,0,1:T(8,128)(2,1)}, u32[]{:S(2)}) copy-start(bf16[8,81,81]{2,0,1:T(8,128)(2,1)} %param.19) | copy-start | bytes 314932
  0.0 12.7 %copy-start.6 = (bf16[81,81]{1,0:T(8,128)(2,1)S(1)}, bf16[81,81]{1,0:T(8,128)(2,1)}, u32[]{:S(2)}) copy-start(bf16[81,81]{1,0:T(8,128)(2,1)} %param.23) | copy-start | bytes 39370
  0.0 14.9 %copy-start.5 = (s32[26,4,4,2]{0,3,2,1:T(2,128)S(1)}, s32[26,4,4,2]{0,3,2,1:T(2,128)}, u32[]{:S(2)}) copy-start(s32[26,4,4,2]{0,3,2,1:T(2,128)} %param.18) | copy-start | bytes 9988
  8.1 14.7 %collective-permute-start.1 = (f32[5068]{0:T(1024)S(1)}, f32[5068]{0:T(1024)S(1)}, u32[]{:S(2)}, u32[]{:S(2)}) collective-permute-start(f32[5068]{0:T(1024)S(1)} %concatenate.99), channel_id=1, source_target_pairs={{8,0},{16,8},{24,16},{0,24},{9,1},{17,9},{25,17},{1,25},{10,2},{18... | collective-permute-start | bytes 60824 | tf_op jit(solution)/shard_map/ppermute | solution.py:36
  12.4 10.7 %collective-permute-start = (f32[5068]{0:T(1024)S(1)}, f32[5068]{0:T(1024)S(1)}, u32[]{:S(2)}, u32[]{:S(2)}) collective-permute-start(f32[5068]{0:T(1024)S(1)} %concatenate.98), channel_id=1, source_target_pairs={{0,8},{8,16},{16,24},{24,0},{1,9},{9,17},{17,25},{25,1},{2,10},{10... | collective-permute-start | bytes 60824 | tf_op jit(solution)/shard_map/ppermute | solution.py:35
  12.8 14.6 %collective-permute-start.4 = (f32[81]{0:T(128)S(1)}, f32[81]{0:T(128)S(1)}, u32[]{:S(2)}, u32[]{:S(2)}) collective-permute-start(f32[81]{0:T(128)S(1)} %bitcast.493), channel_id=1, source_target_pairs={{0,8},{8,0},{16,24},{24,16},{1,9},{9,1},{17,25},{25,17},{2,10},{10... | collective-permute-start | bytes 980 | tf_op jit(solution)/shard_map/ppermute | solution.py:18
  18.0 1.5 %copy-start.2 = (bf16[2,2,81,81]{3,1,2,0:T(2,128)(2,1)S(1)}, bf16[2,2,81,81]{3,1,2,0:T(2,128)(2,1)}, u32[]{:S(2)}) copy-start(bf16[2,2,81,81]{3,1,2,0:T(2,128)(2,1)} %param.25) | copy-start | bytes 157468
  18.0 1.8 %copy-start.3 = (bf16[2,2,81,81]{3,1,2,0:T(2,128)(2,1)S(1)}, bf16[2,2,81,81]{3,1,2,0:T(2,128)(2,1)}, u32[]{:S(2)}) copy-start(bf16[2,2,81,81]{3,1,2,0:T(2,128)(2,1)} %param.26) | copy-start | bytes 157468
  18.1 1.9 %copy-start.4 = (bf16[2,2,81,81]{3,1,2,0:T(2,128)(2,1)S(1)}, bf16[2,2,81,81]{3,1,2,0:T(2,128)(2,1)}, u32[]{:S(2)}) copy-start(bf16[2,2,81,81]{3,1,2,0:T(2,128)(2,1)} %param.27) | copy-start | bytes 157468
  18.1 2.5 %copy-start.19 = (f32[26]{0:T(128)S(1)}, f32[26]{0:T(128)}, u32[]{:S(2)}) copy-start(f32[26]{0:T(128)} %constant.264) | copy-start | bytes 316
  18.1 2.5 %copy-start.20 = (f32[26]{0:T(128)S(1)}, f32[26]{0:T(128)}, u32[]{:S(2)}) copy-start(f32[26]{0:T(128)} %constant.262) | copy-start | bytes 316
  18.1 2.5 %copy-start.21 = (f32[26]{0:T(128)S(1)}, f32[26]{0:T(128)}, u32[]{:S(2)}) copy-start(f32[26]{0:T(128)} %constant.260) | copy-start | bytes 316
  18.1 2.7 %copy-start.16 = (f32[98]{0:T(128)S(1)}, f32[98]{0:T(128)}, u32[]{:S(2)}) copy-start(f32[98]{0:T(128)} %constant.258) | copy-start | bytes 1180
  18.1 2.7 %copy-start.17 = (f32[98]{0:T(128)S(1)}, f32[98]{0:T(128)}, u32[]{:S(2)}) copy-start(f32[98]{0:T(128)} %constant.256) | copy-start | bytes 1180
  18.1 2.7 %copy-start.18 = (f32[98]{0:T(128)S(1)}, f32[98]{0:T(128)}, u32[]{:S(2)}) copy-start(f32[98]{0:T(128)} %constant.254) | copy-start | bytes 1180
  25.0 10.1 %copy-start.15 = (f32[27,8]{1,0:T(8,128)S(1)}, f32[27,8]{1,0:T(8,128)}, u32[]{:S(2)}) copy-start(f32[27,8]{1,0:T(8,128)} %constant.241.clone) | copy-start | bytes 2596
  25.2 4.0 %collective-permute-start.3 = (f32[8088]{0:T(1024)S(1)}, f32[8088]{0:T(1024)S(1)}, u32[]{:S(2)}, u32[]{:S(2)}) collective-permute-start(f32[8088]{0:T(1024)S(1)} %concatenate.104), channel_id=1, source_target_pairs={{1,0},{2,1},{3,2},{4,3},{5,4},{6,5},{7,6},{0,7},{9,8},{10,9},{11,1... | collective-permute-start | bytes 97064 | tf_op jit(solution)/shard_map/ppermute | solution.py:36
  28.4 5.3 %collective-permute-start.2 = (f32[8088]{0:T(1024)S(1)}, f32[8088]{0:T(1024)S(1)}, u32[]{:S(2)}, u32[]{:S(2)}) collective-permute-start(f32[8088]{0:T(1024)S(1)} %concatenate.103), channel_id=1, source_target_pairs={{0,1},{1,2},{2,3},{3,4},{4,5},{5,6},{6,7},{7,0},{8,9},{9,10},{10,1... | collective-permute-start | bytes 97064 | tf_op jit(solution)/shard_map/ppermute | solution.py:35
  46.1 25.2 %collective-permute-start.5 = (f32[81]{0:T(128)S(1)}, f32[81]{0:T(128)S(1)}, u32[]{:S(2)}, u32[]{:S(2)}) collective-permute-start(f32[81]{0:T(128)S(1)} %fusion.12), channel_id=1, source_target_pairs={{0,16},{8,24},{16,0},{24,8},{1,17},{9,25},{17,1},{25,9},{2,18},{10... | collective-permute-start | bytes 980 | tf_op jit(solution)/shard_map/ppermute | solution.py:18
  55.3 7.3 %copy-start.13 = (f32[4,8,128]{2,1,0:T(8,128)S(1)}, f32[4,8,128]{2,1,0:T(8,128)}, u32[]{:S(2)}) copy-start(f32[4,8,128]{2,1,0:T(8,128)} %shard_map.155) | copy-start | bytes 49156
  71.2 20.5 %copy-start.12 = (f32[4,8,128]{2,1,0:T(8,128)S(1)}, f32[4,8,128]{2,1,0:T(8,128)}, u32[]{:S(2)}) copy-start(f32[4,8,128]{2,1,0:T(8,128)} %shard_map.159) | copy-start | bytes 49156
  71.2 20.5 %copy-start.11 = (f32[4,8,128]{2,1,0:T(8,128)S(1)}, f32[4,8,128]{2,1,0:T(8,128)}, u32[]{:S(2)}) copy-start(f32[4,8,128]{2,1,0:T(8,128)} %shard_map.160) | copy-start | bytes 49156
  71.2 20.5 %copy-start.14 = (f32[4,8,128]{2,1,0:T(8,128)S(1)}, f32[4,8,128]{2,1,0:T(8,128)}, u32[]{:S(2)}) copy-start(f32[4,8,128]{2,1,0:T(8,128)} %shard_map.161) | copy-start | bytes 49156
  71.2 25.3 %copy-start.7 = (bf16[81,81]{1,0:T(8,128)(2,1)S(1)}, bf16[81,81]{1,0:T(8,128)(2,1)}, u32[]{:S(2)}) copy-start(bf16[81,81]{1,0:T(8,128)(2,1)} %param.28) | copy-start | bytes 39370
  71.3 27.1 %copy-start.8 = (bf16[81,81]{1,0:T(8,128)(2,1)S(1)}, bf16[81,81]{1,0:T(8,128)(2,1)}, u32[]{:S(2)}) copy-start(bf16[81,81]{1,0:T(8,128)(2,1)} %param.24) | copy-start | bytes 39370
  71.3 27.5 %copy-start.9 = (bf16[81,81]{1,0:T(8,128)(2,1)S(1)}, bf16[81,81]{1,0:T(8,128)(2,1)}, u32[]{:S(2)}) copy-start(bf16[81,81]{1,0:T(8,128)(2,1)} %param.22) | copy-start | bytes 39370
  71.3 27.7 %copy-start.1 = (bf16[8,81,81]{2,0,1:T(8,128)(2,1)S(1)}, bf16[8,81,81]{2,0,1:T(8,128)(2,1)}, u32[]{:S(2)}) copy-start(bf16[8,81,81]{2,0,1:T(8,128)(2,1)} %param.20) | copy-start | bytes 314932
  76.2 23.3 %copy-start.10 = (bf16[81,81]{1,0:T(8,128)(2,1)S(1)}, bf16[81,81]{1,0:T(8,128)(2,1)}, u32[]{:S(2)}) copy-start(bf16[81,81]{1,0:T(8,128)(2,1)} %param.21) | copy-start | bytes 39370
  76.3 1.2 %collective-permute-start.6 = (f32[81]{0:T(128)S(1)}, f32[81]{0:T(128)S(1)}, u32[]{:S(2)}, u32[]{:S(2)}) collective-permute-start(f32[81]{0:T(128)S(1)} %fusion.11), channel_id=1, source_target_pairs={{0,1},{1,0},{2,3},{3,2},{4,5},{5,4},{6,7},{7,6},{8,9},{9,8},{10,11... | collective-permute-start | bytes 980 | tf_op jit(solution)/shard_map/ppermute | solution.py:18
  82.4 3.6 %collective-permute-start.7 = (f32[81]{0:T(128)S(1)}, f32[81]{0:T(128)S(1)}, u32[]{:S(2)}, u32[]{:S(2)}) collective-permute-start(f32[81]{0:T(128)S(1)} %fusion.10), channel_id=1, source_target_pairs={{0,2},{1,3},{2,0},{3,1},{4,6},{5,7},{6,4},{7,5},{8,10},{9,11},{10,... | collective-permute-start | bytes 980 | tf_op jit(solution)/shard_map/ppermute | solution.py:18
  91.9 4.5 %collective-permute-start.8 = (f32[81]{0:T(128)S(1)}, f32[81]{0:T(128)S(1)}, u32[]{:S(2)}, u32[]{:S(2)}) collective-permute-start(f32[81]{0:T(128)S(1)} %fusion.9), channel_id=1, source_target_pairs={{0,4},{1,5},{2,6},{3,7},{4,0},{5,1},{6,2},{7,3},{8,12},{9,13},{10,... | collective-permute-start | bytes 980 | tf_op jit(solution)/shard_map/ppermute | solution.py:18
where the time goes:
time: 104 us
  Pallas kernels  41.7 us (40%)
  local copies, waits for them, and re-layouts  19.8 us (19%)
  other arithmetic  13.2 us (13%)
  waiting for transfers between devices  11.8 us (11%)
  starting transfers between devices  11.2 us (11%)
  matrix products  4.48 us (4%)
  between operations  1.56 us (2%)
    pallas_call x8, Pallas kernels, run_piece(): pl.pallas_call(functools.partial(near_kernel, first_leaf, leaf_count, wid...  41.7 us
    ppermute x5, waiting for transfers between devices, from_partner(): return lax.ppermute(value, axis, pairs)  7.21 us
    ppermute x2, starting transfers between devices, extended_joint(): lax.ppermute(jnp.concatenate([piece.reshape(-1) for piece in highs]), axi...  6.1 us
    unnamed x168, local copies, waits for them, and re-layouts  4.99 us
    ppermute x5, starting transfers between devices, from_partner(): return lax.ppermute(value, axis, pairs)  4.93 us
    ppermute x2, waiting for transfers between devices, extended_joint(): lax.ppermute(jnp.concatenate([piece.reshape(-1) for piece in lows]), axis...  4.16 us
    dot_general x23, matrix products, matrix_vector(): return jnp.dot(matrix, vector, precision=highest)  3.38 us
    reduce_sum x1, other arithmetic, evaluate(): jnp.sum(cos_local * cosine + sin_local * sine_part, axis=0)  2.97 us
  transfers between devices with their start and end apart: 9, of which 5 were waited for; matrix products, arithmetic and copies ran while one was open for 18% of the time, Pallas kernels for 17%

commit v1 on v0

--- a/solution.py
+++ b/solution.py
@@ -43,6 +43,49 @@
             grown.append(jnp.concatenate([low, b, high], axis=dim))
         blocks = grown
     return blocks
+
+
+def extended_once(parts):
+    count_x, count_y = lax.axis_size("gx"), lax.axis_size("gy")
+    received = {}
+    for step_x in (-1, 0, 1):
+        for step_y in (-1, 0, 1):
+            if (step_x, step_y) == (0, 0):
+                continue
+            sends = []
+            for block, width in parts:
+                size_x, size_y = block.shape[1], block.shape[2]
+                range_x = (size_x - width, size_x) if step_x < 0 else (0, width) if step_x > 0 else (0, size_x)
+                range_y = (size_y - width, size_y) if step_y < 0 else (0, width) if step_y > 0 else (0, size_y)
+                sends.append(block[:, range_x[0] : range_x[1], range_y[0] : range_y[1]])
+            flat = jnp.concatenate([piece.reshape(-1) for piece in sends])
+            if step_y == 0:
+                pairs = [(i, (i - step_x) % count_x) for i in range(count_x)]
+                flat = lax.ppermute(flat, "gx", pairs)
+            elif step_x == 0:
+                pairs = [(j, (j - step_y) % count_y) for j in range(count_y)]
+                flat = lax.ppermute(flat, "gy", pairs)
+            else:
+                pairs = [
+                    (i * count_y + j, ((i - step_x) % count_x) * count_y + (j - step_y) % count_y)
+                    for i in range(count_x)
+                    for j in range(count_y)
+                ]
+                flat = lax.ppermute(flat, ("gx", "gy"), pairs)
+            place = 0
+            pieces = []
+            for piece in sends:
+                pieces.append(flat[place : place + piece.size].reshape(piece.shape))
+                place += piece.size
+            received[(step_x, step_y)] = pieces
+    grown = []
+    for number, (block, width) in enumerate(parts):
+        bands = []
+        for step_x in (-1, 0, 1):
+            row = [block if (step_x, step_y) == (0, 0) else received[(step_x, step_y)][number] for step_y in (-1, 0, 1)]
+            bands.append(jnp.concatenate(row, axis=2))
+        grown.append(jnp.concatenate(bands, axis=1))
+    return grown
 
 
 def wave_table(coef_count, float_type):
@@ -459,7 +502,7 @@
     half_count = waves.shape[1]
     moments = leaf_moments(charged, waves)
     parents = climb_children(moments, child_up.astype(jnp.float32))
-    rimmed, parent_rim, leaf_rim = extended_joint([(charged, 1), (parents, 2), (moments, 1)], (("gx", 1), ("gy", 2)))
+    rimmed, parent_rim, leaf_rim = extended_once([(charged, 1), (parents, 2), (moments, 1)])
     parent_rim = jnp.pad(parent_rim, ((0, 0), (0, 0), (0, 0), (2, 2)))
     half_x, half_y, half_z = (parents.shape[1], parents.shape[2], parents.shape[3])
     phase_grid = block_phase(waves, half_x, half_y, half_z, jnp.float32)

time: 104 us -> 119 us (1.14)
  waiting for transfers between devices: 11.8 us -> 18.3 us
  local copies, waits for them, and re-layouts: 19.8 us -> 24.8 us
  starting transfers between devices: 11.2 us -> 13.5 us
  Pallas kernels: 41.7 us -> 43.7 us
    ppermute x4 -> x8, waiting for transfers between devices: 4.58 us -> 11 us  [the longest x4 9.52 us: extended_once(): flat = lax.ppermute(flat, ('gx', 'gy'), pairs)]
    ppermute x4 -> x8, starting transfers between devices: 6.28 us -> 12 us  [the longest x4 6.39 us: extended_once(): flat = lax.ppermute(flat, ('gx', 'gy'), pairs)]
    ppermute x5, starting transfers between devices: 4.93 us -> 1.44 us  [from_partner(): return lax.ppermute(value, axis, pairs)]
    reshape x22 -> x43, local copies, waits for them, and re-layouts: 3.27 us -> 6.05 us  [the longest x34 4.61 us: extended_once(): pieces.append(flat[place:place + piece.size].reshape(piece.shape))]
    pallas_call x8, Pallas kernels: 41.7 us -> 43.7 us  [run_piece(): pl.pallas_call(functools.partial(near_kernel, first_leaf, leaf_count, wid...]
    another operation x5 -> x17, local copies, waits for them, and re-layouts: 0.53 us -> 2.1 us  [body(): jnp.stack([parent_rim[:, 2 + offset[0]:2 + offset[0] + half_x, 2 + offset...]
    unnamed x168 -> x166, local copies, waits for them, and re-layouts: 4.99 us -> 4.98 us
  transfers between devices with their start and end apart: 9 -> 13, of which waited for: 5 -> 6; matrix products, arithmetic and copies ran while one was open for 18% -> 18% of each run, Pallas kernels for 17% -> 14%
where the time goes in v1:
time: 119 us; the launch traced here: 120 us
  Pallas kernels  43.7 us (37%)
  local copies, waits for them, and re-layouts  24.8 us (21%)
  waiting for transfers between devices  18.3 us (15%)
  starting transfers between devices  13.5 us (11%)
  other arithmetic  13.2 us (11%)
  matrix products  4.49 us (4%)
  between operations  1.61 us (1%)
    pallas_call x8, Pallas kernels, run_piece(): pl.pallas_call(functools.partial(near_kernel, first_leaf, leaf_count, wid...  43.7 us
    ppermute x4, waiting for transfers between devices, extended_once(): flat = lax.ppermute(flat, ('gx', 'gy'), pairs)  9.52 us
    ppermute x5, waiting for transfers between devices, from_partner(): return lax.ppermute(value, axis, pairs)  7.21 us
    ppermute x4, starting transfers between devices, extended_once(): flat = lax.ppermute(flat, ('gx', 'gy'), pairs)  6.39 us
    ppermute x2, starting transfers between devices, extended_once(): flat = lax.ppermute(flat, 'gy', pairs)  5.11 us
    unnamed x166, local copies, waits for them, and re-layouts  4.98 us
    reshape x34, local copies, waits for them, and re-layouts, extended_once(): pieces.append(flat[place:place + piece.size].reshape(piece.shape))  4.61 us
    dot_general x23, matrix products, matrix_vector(): return jnp.dot(matrix, vector, precision=highest)  3.39 us
  transfers between devices with their start and end apart: 13, of which 6 were waited for; matrix products, arithmetic and copies ran while one was open for 18% of the time, Pallas kernels for 14%

profile of v1, /device:TPU:0, one launch (start us, length us, event | category | flops | bytes accessed | tf_op | source)
XLA Modules:
  0.0 119.6 jit_solution(8456402066782243374)
XLA Ops:
  0.1 0.8 copy.410
  0.9 0.8 slice.631
  1.7 0.9 add_bitcast_fusion.2
  2.6 0.9 fusion.38
  3.5 2.9 %multiply_reduce_fusion.4 = (f32[40,4,4,2]{0,3,2,1:T(2,128)S(1)}, f32[40,4,4,2]{0,3,2,1:T(2,128)S(1)}) fusion(f32[4,4,2,128]{3,2,1,0:T(2,128)S(1)} %bitcast.443, f32[4,4,2,128]{3,2,1,0:T(2,128)S(1)} %get-tuple-element.79, f32[40]{0:T(128)S(1)} %get-tuple-element.135, f32[4,4,2,128]{3,2,1,0:T(2,128)S(1)} %get-tuple-element.80, f32[40]{0:T(128)S(1)} %get-tuple-element.136, ...), kind=kLoop, calls=%fused_computation.50 | loop fusion | flops 1472000 | bytes 76256 | tf_op jit(solution)/shard_map/reduce_sum | solution.py:153
  8.0 6.4 %collective-permute-start.7 = (f32[1510]{0:T(1024)S(1)}, f32[1510]{0:T(1024)S(1)}, u32[]{:S(2)}, u32[]{:S(2)}) collective-permute-start(f32[1510]{0:T(1024)S(1)} %concatenate.149), channel_id=1, source_target_pairs={{0,31},{1,24},{2,25},{3,26},{4,27},{5,28},{6,29},{7,30},{8,7},{9,0... | collective-permute-start | bytes 18128 | tf_op jit(solution)/shard_map/ppermute | solution.py:74
  16.1 4.4 %collective-permute-start.4 = (f32[5068]{0:T(1024)S(1)}, f32[5068]{0:T(1024)S(1)}, u32[]{:S(2)}, u32[]{:S(2)}) collective-permute-start(f32[5068]{0:T(1024)S(1)} %concatenate.145), channel_id=1, source_target_pairs={{0,7},{1,0},{2,1},{3,2},{4,3},{5,4},{6,5},{7,6},{8,15},{9,8},{10,9... | collective-permute-start | bytes 60824 | tf_op jit(solution)/shard_map/ppermute | solution.py:67
  25.4 1.4 %fusion.99 = (f32[4,128,4]{2,1,0:T(8,128)}, f32[4,128,4]{2,1,0:T(8,128)}, f32[4,128,4]{2,1,0:T(8,128)}, f32[4,128,4]{2,1,0:T(8,128)}, f32[4,128,4]{2,1,0:T(8,128...) fusion(f32[32,128,4]{2,1,0:T(8,128)S(1)} %bitcast.440), kind=kLoop, calls=%fused_computation.471 | loop fusion | bytes 131072 | tf_op jit(solution)/shard_map/slice | solution.py:457
  30.4 0.7 concatenate.133.table_ref
  31.2 6.6 %collective-permute-done = f32[1510]{0:T(1024)S(1)} collective-permute-done((f32[1510]{0:T(1024)S(1)}, f32[1510]{0:T(1024)S(1)}, u32[]{:S(2)}, u32[]{:S(2)}) %collective-permute-start) | collective-permute-done | bytes 6072 | tf_op jit(solution)/shard_map/ppermute | solution.py:74
  38.1 0.7 collective-permute-start.3
  38.8 3.0 %collective-permute-done.2 = f32[1510]{0:T(1024)S(1)} collective-permute-done((f32[1510]{0:T(1024)S(1)}, f32[1510]{0:T(1024)S(1)}, u32[]{:S(2)}, u32[]{:S(2)}) %collective-permute-start.2) | collective-permute-done | bytes 6072 | tf_op jit(solution)/shard_map/ppermute | solution.py:74
  44.9 1.5 %collective-permute-done.1 = f32[5068]{0:T(1024)S(1)} collective-permute-done((f32[5068]{0:T(1024)S(1)}, f32[5068]{0:T(1024)S(1)}, u32[]{:S(2)}, u32[]{:S(2)}) %collective-permute-start.1) | collective-permute-done | bytes 20304 | tf_op jit(solution)/shard_map/ppermute | solution.py:64
  50.2 0.7 pad.11.source_ref
  51.0 0.7 broadcast_in_dim.44.shift_ref
  51.7 5.6 %shard_map.154 = f32[4,8,128]{2,1,0:T(8,128)} custom-call(s32[1792]{0:T(1024)} %concatenate.133.table_ref, f32[4,128,4]{2,1,0:T(8,128)} %get-tuple-element.36.target_ref, f32[73,8,128]{2,1,0:T(8,128)} %pad.11.source_ref, f32[27,8,128]{2,1,0:T(8,128)} %broadcast_in_dim.44.shift_ref), custom_call_target="tpu_custom_call" | custom-call | flops 13107200 | bytes 524288 | tf_op jit(solution)/shard_map/pallas_call | solution.py:460
  57.3 0.7 constant_dynamic-update-slice_fusion.7
  58.1 5.4 %shard_map.155 = f32[4,8,128]{2,1,0:T(8,128)} custom-call(s32[1792]{0:T(1024)} %concatenate.133.table_ref, f32[4,128,4]{2,1,0:T(8,128)} %get-tuple-element.13.target_ref, f32[73,8,128]{2,1,0:T(8,128)} %pad.11.source_ref, f32[27,8,128]{2,1,0:T(8,128)} %broadcast_in_dim.44.shift_ref), custom_call_target="tpu_custom_call" | custom-call | flops 13107200 | bytes 524288 | tf_op jit(solution)/shard_map/pallas_call | solution.py:460
  63.5 0.8 collective-permute-start.9
  64.3 5.8 %shard_map.159 = f32[4,8,128]{2,1,0:T(8,128)} custom-call(s32[1792]{0:T(1024)} %concatenate.133.table_ref, f32[4,128,4]{2,1,0:T(8,128)} %get-tuple-element.31.target_ref, f32[73,8,128]{2,1,0:T(8,128)} %pad.11.source_ref, f32[27,8,128]{2,1,0:T(8,128)} %broadcast_in_dim.44.shift_ref), custom_call_target="tpu_custom_call" | custom-call | flops 13107200 | bytes 524288 | tf_op jit(solution)/shard_map/pallas_call | solution.py:460
  70.2 5.4 %shard_map.160 = f32[4,8,128]{2,1,0:T(8,128)} custom-call(s32[1792]{0:T(1024)} %concatenate.133.table_ref, f32[4,128,4]{2,1,0:T(8,128)} %get-tuple-element.30.target_ref, f32[73,8,128]{2,1,0:T(8,128)} %pad.11.source_ref, f32[27,8,128]{2,1,0:T(8,128)} %broadcast_in_dim.44.shift_ref), custom_call_target="tpu_custom_call" | custom-call | flops 13107200 | bytes 524288 | tf_op jit(solution)/shard_map/pallas_call | solution.py:460
  80.3 5.3 %shard_map.161 = f32[4,8,128]{2,1,0:T(8,128)} custom-call(s32[1792]{0:T(1024)} %concatenate.133.table_ref, f32[4,128,4]{2,1,0:T(8,128)} %get-tuple-element.29.target_ref, f32[73,8,128]{2,1,0:T(8,128)} %pad.11.source_ref, f32[27,8,128]{2,1,0:T(8,128)} %broadcast_in_dim.44.shift_ref), custom_call_target="tpu_custom_call" | custom-call | flops 13107200 | bytes 524288 | tf_op jit(solution)/shard_map/pallas_call | solution.py:460
  85.6 5.2 %shard_map.156 = f32[4,8,128]{2,1,0:T(8,128)} custom-call(s32[1792]{0:T(1024)} %concatenate.133.table_ref, f32[4,128,4]{2,1,0:T(8,128)} %get-tuple-element.15.target_ref, f32[73,8,128]{2,1,0:T(8,128)} %pad.11.source_ref, f32[27,8,128]{2,1,0:T(8,128)} %broadcast_in_dim.44.shift_ref), custom_call_target="tpu_custom_call" | custom-call | flops 13107200 | bytes 524288 | tf_op jit(solution)/shard_map/pallas_call | solution.py:460
  91.1 0.8 constant_dynamic-update-slice_fusion.5
  92.1 5.9 %shard_map.157 = f32[4,8,128]{2,1,0:T(8,128)} custom-call(s32[1792]{0:T(1024)} %concatenate.133.table_ref, f32[4,128,4]{2,1,0:T(8,128)} %get-tuple-element.17.target_ref, f32[73,8,128]{2,1,0:T(8,128)} %pad.11.source_ref, f32[27,8,128]{2,1,0:T(8,128)} %broadcast_in_dim.44.shift_ref), custom_call_target="tpu_custom_call" | custom-call | flops 13107200 | bytes 524288 | tf_op jit(solution)/shard_map/pallas_call | solution.py:460
  98.3 0.8 constant_dynamic-update-slice_fusion.4
  99.1 2.7 %collective-permute-done.11 = f32[81]{0:T(128)S(1)} collective-permute-done((f32[81]{0:T(128)S(1)}, f32[81]{0:T(128)S(1)}, u32[]{:S(2)}, u32[]{:S(2)}) %collective-permute-start.11) | collective-permute-done | bytes 356 | tf_op jit(solution)/shard_map/ppermute | solution.py:18
  101.7 5.1 %shard_map.158 = f32[4,8,128]{2,1,0:T(8,128)} custom-call(s32[1792]{0:T(1024)} %concatenate.133.table_ref, f32[4,128,4]{2,1,0:T(8,128)} %get-tuple-element.19.target_ref, f32[73,8,128]{2,1,0:T(8,128)} %pad.11.source_ref, f32[27,8,128]{2,1,0:T(8,128)} %broadcast_in_dim.44.shift_ref), custom_call_target="tpu_custom_call" | custom-call | flops 13107200 | bytes 524288 | tf_op jit(solution)/shard_map/pallas_call | solution.py:460
  106.8 0.7 constant_dynamic-update-slice_fusion.3
  107.9 4.3 %collective-permute-done.12 = f32[81]{0:T(128)S(1)} collective-permute-done((f32[81]{0:T(128)S(1)}, f32[81]{0:T(128)S(1)}, u32[]{:S(2)}, u32[]{:S(2)}) %collective-permute-start.12) | collective-permute-done | bytes 356 | tf_op jit(solution)/shard_map/ppermute | solution.py:18
  115.8 3.0 %add_reduce_fusion = (f32[4,4,2,128]{3,2,1,0:T(2,128)S(1)}, f32[4,4,2,128]{3,2,1,0:T(2,128)S(1)}, f32[4,4,2,128]{3,2,1,0:T(2,128)S(1)}, f32[4,4,2,128]{3,2,1,0:T(2,128)S(1)}) fusion(f32[40,4,4,2]{0,3,2,1:T(2,128)S(1)} %get-tuple-element.113, f32[40,4,4,2]{0,3,2,1:T(2,128)S(1)} %get-tuple-element.112, f32[4,4,2,128]{3,2,1,0:T(2,128)S(1)} %get-tuple-element.79, ...), kind=kLoop, calls=%fused_computation.48 | loop fusion | flops 2932736 | bytes 125408 | tf_op jit(solution)/shard_map/reduce_sum | solution.py:165
  118.9 0.7 pad_maximum_fusion.1
  (427 shorter events, 27.6 us)
Async XLA Ops:
  0.0 6.7 %copy-start = (bf16[8,81,81]{2,0,1:T(8,128)(2,1)S(1)}, bf16[8,81,81]{2,0,1:T(8,128)(2,1)}, u32[]{:S(2)}) copy-start(bf16[8,81,81]{2,0,1:T(8,128)(2,1)} %param.19) | copy-start | bytes 314932
  0.0 20.8 %copy-start.6 = (bf16[81,81]{1,0:T(8,128)(2,1)S(1)}, bf16[81,81]{1,0:T(8,128)(2,1)}, u32[]{:S(2)}) copy-start(bf16[81,81]{1,0:T(8,128)(2,1)} %param.23) | copy-start | bytes 39370
  0.0 21.8 %copy-start.5 = (s32[26,4,4,2]{0,3,2,1:T(2,128)S(1)}, s32[26,4,4,2]{0,3,2,1:T(2,128)}, u32[]{:S(2)}) copy-start(s32[26,4,4,2]{0,3,2,1:T(2,128)} %param.18) | copy-start | bytes 9988
  8.0 34.6 %collective-permute-start.7 = (f32[1510]{0:T(1024)S(1)}, f32[1510]{0:T(1024)S(1)}, u32[]{:S(2)}, u32[]{:S(2)}) collective-permute-start(f32[1510]{0:T(1024)S(1)} %concatenate.149), channel_id=1, source_target_pairs={{0,31},{1,24},{2,25},{3,26},{4,27},{5,28},{6,29},{7,30},{8,7},{9,0... | collective-permute-start | bytes 18128 | tf_op jit(solution)/shard_map/ppermute | solution.py:74
  14.8 32.7 %collective-permute-start.6 = (f32[5068]{0:T(1024)S(1)}, f32[5068]{0:T(1024)S(1)}, u32[]{:S(2)}, u32[]{:S(2)}) collective-permute-start(f32[5068]{0:T(1024)S(1)} %concatenate.148), channel_id=1, source_target_pairs={{0,24},{8,0},{16,8},{24,16},{1,25},{9,1},{17,9},{25,17},{2,26},{10... | collective-permute-start | bytes 60824 | tf_op jit(solution)/shard_map/ppermute | solution.py:64
  15.7 22.4 %collective-permute-start.5 = (f32[1510]{0:T(1024)S(1)}, f32[1510]{0:T(1024)S(1)}, u32[]{:S(2)}, u32[]{:S(2)}) collective-permute-start(f32[1510]{0:T(1024)S(1)} %concatenate.147), channel_id=1, source_target_pairs={{0,25},{1,26},{2,27},{3,28},{4,29},{5,30},{6,31},{7,24},{8,1},{9,2... | collective-permute-start | bytes 18128 | tf_op jit(solution)/shard_map/ppermute | solution.py:74
  16.1 31.0 %collective-permute-start.4 = (f32[5068]{0:T(1024)S(1)}, f32[5068]{0:T(1024)S(1)}, u32[]{:S(2)}, u32[]{:S(2)}) collective-permute-start(f32[5068]{0:T(1024)S(1)} %concatenate.145), channel_id=1, source_target_pairs={{0,7},{1,0},{2,1},{3,2},{4,3},{5,4},{6,5},{7,6},{8,15},{9,8},{10,9... | collective-permute-start | bytes 60824 | tf_op jit(solution)/shard_map/ppermute | solution.py:67
  20.9 10.1 %collective-permute-start.8 = (f32[81]{0:T(128)S(1)}, f32[81]{0:T(128)S(1)}, u32[]{:S(2)}, u32[]{:S(2)}) collective-permute-start(f32[81]{0:T(128)S(1)} %bitcast.483), channel_id=1, source_target_pairs={{0,8},{8,0},{16,24},{24,16},{1,9},{9,1},{17,25},{25,17},{2,10},{10... | collective-permute-start | bytes 980 | tf_op jit(solution)/shard_map/ppermute | solution.py:18
  25.3 3.1 %copy-start.19 = (f32[98]{0:T(128)S(1)}, f32[98]{0:T(128)}, u32[]{:S(2)}) copy-start(f32[98]{0:T(128)} %constant.256) | copy-start | bytes 1180
  25.3 3.1 %copy-start.20 = (f32[98]{0:T(128)S(1)}, f32[98]{0:T(128)}, u32[]{:S(2)}) copy-start(f32[98]{0:T(128)} %constant.254) | copy-start | bytes 1180
  25.4 3.4 %copy-start.3 = (bf16[2,2,81,81]{3,1,2,0:T(2,128)(2,1)S(1)}, bf16[2,2,81,81]{3,1,2,0:T(2,128)(2,1)}, u32[]{:S(2)}) copy-start(bf16[2,2,81,81]{3,1,2,0:T(2,128)(2,1)} %param.26) | copy-start | bytes 157468
  25.4 3.5 %copy-start.4 = (bf16[2,2,81,81]{3,1,2,0:T(2,128)(2,1)S(1)}, bf16[2,2,81,81]{3,1,2,0:T(2,128)(2,1)}, u32[]{:S(2)}) copy-start(bf16[2,2,81,81]{3,1,2,0:T(2,128)(2,1)} %param.27) | copy-start | bytes 157468
  26.7 3.1 %copy-start.16 = (f32[26]{0:T(128)S(1)}, f32[26]{0:T(128)}, u32[]{:S(2)}) copy-start(f32[26]{0:T(128)} %constant.262) | copy-start | bytes 316
  26.7 3.1 %copy-start.17 = (f32[26]{0:T(128)S(1)}, f32[26]{0:T(128)}, u32[]{:S(2)}) copy-start(f32[26]{0:T(128)} %constant.260) | copy-start | bytes 316
  31.1 6.7 %collective-permute-start = (f32[1510]{0:T(1024)S(1)}, f32[1510]{0:T(1024)S(1)}, u32[]{:S(2)}, u32[]{:S(2)}) collective-permute-start(f32[1510]{0:T(1024)S(1)} %concatenate.140), channel_id=1, source_target_pairs={{0,9},{1,10},{2,11},{3,12},{4,13},{5,14},{6,15},{7,8},{8,17},{9,18... | collective-permute-start | bytes 18128 | tf_op jit(solution)/shard_map/ppermute | solution.py:74
  37.7 4.0 %collective-permute-start.2 = (f32[1510]{0:T(1024)S(1)}, f32[1510]{0:T(1024)S(1)}, u32[]{:S(2)}, u32[]{:S(2)}) collective-permute-start(f32[1510]{0:T(1024)S(1)} %concatenate.142), channel_id=1, source_target_pairs={{0,15},{1,8},{2,9},{3,10},{4,11},{5,12},{6,13},{7,14},{8,23},{9,16... | collective-permute-start | bytes 18128 | tf_op jit(solution)/shard_map/ppermute | solution.py:74
  38.1 8.7 %collective-permute-start.3 = (f32[5068]{0:T(1024)S(1)}, f32[5068]{0:T(1024)S(1)}, u32[]{:S(2)}, u32[]{:S(2)}) collective-permute-start(f32[5068]{0:T(1024)S(1)} %concatenate.144), channel_id=1, source_target_pairs={{0,1},{1,2},{2,3},{3,4},{4,5},{5,6},{6,7},{7,0},{8,9},{9,10},{10,1... | collective-permute-start | bytes 60824 | tf_op jit(solution)/shard_map/ppermute | solution.py:67
  41.7 4.7 %collective-permute-start.1 = (f32[5068]{0:T(1024)S(1)}, f32[5068]{0:T(1024)S(1)}, u32[]{:S(2)}, u32[]{:S(2)}) collective-permute-start(f32[5068]{0:T(1024)S(1)} %concatenate.141), channel_id=1, source_target_pairs={{0,8},{8,16},{16,24},{24,0},{1,9},{9,17},{17,25},{25,1},{2,10},{10... | collective-permute-start | bytes 60824 | tf_op jit(solution)/shard_map/ppermute | solution.py:64
  44.0 6.9 %copy-start.14 = (f32[27,8]{1,0:T(8,128)S(1)}, f32[27,8]{1,0:T(8,128)}, u32[]{:S(2)}) copy-start(f32[27,8]{1,0:T(8,128)} %constant.241.clone) | copy-start | bytes 2596
  63.5 22.1 %collective-permute-start.9 = (f32[81]{0:T(128)S(1)}, f32[81]{0:T(128)S(1)}, u32[]{:S(2)}, u32[]{:S(2)}) collective-permute-start(f32[81]{0:T(128)S(1)} %fusion.12), channel_id=1, source_target_pairs={{0,16},{8,24},{16,0},{24,8},{1,17},{9,25},{17,1},{25,9},{2,18},{10... | collective-permute-start | bytes 980 | tf_op jit(solution)/shard_map/ppermute | solution.py:18
  64.3 13.2 %copy-start.12 = (f32[4,8,128]{2,1,0:T(8,128)S(1)}, f32[4,8,128]{2,1,0:T(8,128)}, u32[]{:S(2)}) copy-start(f32[4,8,128]{2,1,0:T(8,128)} %shard_map.155) | copy-start | bytes 49156
  85.6 22.0 %copy-start.11 = (f32[4,8,128]{2,1,0:T(8,128)S(1)}, f32[4,8,128]{2,1,0:T(8,128)}, u32[]{:S(2)}) copy-start(f32[4,8,128]{2,1,0:T(8,128)} %shard_map.159) | copy-start | bytes 49156
  85.6 22.0 %copy-start.10 = (f32[4,8,128]{2,1,0:T(8,128)S(1)}, f32[4,8,128]{2,1,0:T(8,128)}, u32[]{:S(2)}) copy-start(f32[4,8,128]{2,1,0:T(8,128)} %shard_map.160) | copy-start | bytes 49156
  85.6 22.0 %copy-start.13 = (f32[4,8,128]{2,1,0:T(8,128)S(1)}, f32[4,8,128]{2,1,0:T(8,128)}, u32[]{:S(2)}) copy-start(f32[4,8,128]{2,1,0:T(8,128)} %shard_map.161) | copy-start | bytes 49156
  85.6 26.8 %copy-start.7 = (bf16[81,81]{1,0:T(8,128)(2,1)S(1)}, bf16[81,81]{1,0:T(8,128)(2,1)}, u32[]{:S(2)}) copy-start(bf16[81,81]{1,0:T(8,128)(2,1)} %param.28) | copy-start | bytes 39370
  85.6 28.6 %copy-start.8 = (bf16[81,81]{1,0:T(8,128)(2,1)S(1)}, bf16[81,81]{1,0:T(8,128)(2,1)}, u32[]{:S(2)}) copy-start(bf16[81,81]{1,0:T(8,128)(2,1)} %param.24) | copy-start | bytes 39370
  85.6 29.0 %copy-start.9 = (bf16[81,81]{1,0:T(8,128)(2,1)S(1)}, bf16[81,81]{1,0:T(8,128)(2,1)}, u32[]{:S(2)}) copy-start(bf16[81,81]{1,0:T(8,128)(2,1)} %param.22) | copy-start | bytes 39370
  85.6 29.2 %copy-start.1 = (bf16[8,81,81]{2,0,1:T(8,128)(2,1)S(1)}, bf16[8,81,81]{2,0,1:T(8,128)(2,1)}, u32[]{:S(2)}) copy-start(bf16[8,81,81]{2,0,1:T(8,128)(2,1)} %param.20) | copy-start | bytes 314932
  90.8 24.5 %copy-start.21 = (bf16[81,81]{1,0:T(8,128)(2,1)S(1)}, bf16[81,81]{1,0:T(8,128)(2,1)}, u32[]{:S(2)}) copy-start(bf16[81,81]{1,0:T(8,128)(2,1)} %param.21) | copy-start | bytes 39370
  90.9 1.2 collective-permute-start.10
  98.1 3.6 %collective-permute-start.11 = (f32[81]{0:T(128)S(1)}, f32[81]{0:T(128)S(1)}, u32[]{:S(2)}, u32[]{:S(2)}) collective-permute-start(f32[81]{0:T(128)S(1)} %fusion.10), channel_id=1, source_target_pairs={{0,2},{1,3},{2,0},{3,1},{4,6},{5,7},{6,4},{7,5},{8,10},{9,11},{10,... | collective-permute-start | bytes 980 | tf_op jit(solution)/shard_map/ppermute | solution.py:18
  107.8 4.5 %collective-permute-start.12 = (f32[81]{0:T(128)S(1)}, f32[81]{0:T(128)S(1)}, u32[]{:S(2)}, u32[]{:S(2)}) collective-permute-start(f32[81]{0:T(128)S(1)} %fusion.9), channel_id=1, source_target_pairs={{0,4},{1,5},{2,6},{3,7},{4,0},{5,1},{6,2},{7,3},{8,12},{9,13},{10,... | collective-permute-start | bytes 980 | tf_op jit(solution)/shard_map/ppermute | solution.py:18
  (3 other events, 8.7 us)

commit v2 on v0

--- a/solution.py
+++ b/solution.py
@@ -1,6 +1,7 @@
 import functools
 
 import jax
+import numpy as np
 import jax.numpy as jnp
 from jax import lax
 from jax.experimental import pallas as pl
@@ -307,8 +308,13 @@
     return (pair_term, cube_term * delta_x, cube_term * delta_y, cube_term * delta_z)
 
 
-def near_kernel(first_leaf, leaf_count, listed_width, table_ref, target_ref, source_ref, shift_ref, out_ref, tile_ref):
-    piece_leaves = out_ref.shape[0]
+def near_kernel(first_leaf, piece_leaves, leaf_count, listed_width, *refs):
+    if len(refs) == 7:
+        table_ref, target_ref, source_ref, shift_ref, previous_ref, out_ref, tile_ref = refs
+        out_ref[...] = previous_ref[...]
+    else:
+        table_ref, target_ref, source_ref, shift_ref, out_ref, tile_ref = refs
+        out_ref[...] = jnp.zeros(out_ref.shape, out_ref.dtype)
     place_start = 2 * leaf_count
     kind_start = place_start + leaf_count * listed_width
     big = NEAR_ROWS
@@ -364,7 +370,7 @@
         def _():
             chunk_at(last, small)
 
-        out_ref[local] = jnp.transpose(tile_ref[...])[0 : out_ref.shape[1], :]
+        out_ref[leaf] = jnp.transpose(tile_ref[...])[0 : out_ref.shape[1], :]
         return carry
 
     lax.fori_loop(0, piece_leaves, leaf_body, 0)
@@ -379,8 +385,8 @@
     source = jnp.pad(source, ((0, 1), (0, 4), (0, 0)))
     empty_leaf = source.shape[0] - 1
     offsets = [(0, 0, 0)] + leaf_offsets()
-    shift_rows = jnp.array([[float(v) for v in offset] + [0.0] * 5 for offset in offsets], jnp.float32)
-    shift_table = jnp.broadcast_to(shift_rows[:, :, None], (len(offsets), 8, slot_count))
+    shift_rows = np.array([[float(v) for v in offset] + [0.0] * 5 for offset in offsets], np.float32)
+    shift_table = jnp.asarray(np.ascontiguousarray(np.broadcast_to(shift_rows[:, :, None], (len(offsets), 8, slot_count))))
     leaf_x = jnp.arange(size_x, dtype=jnp.int32)[:, None, None]
     leaf_y = jnp.arange(size_y, dtype=jnp.int32)[None, :, None]
     leaf_z = jnp.arange(size_z, dtype=jnp.int32)[None, None, :]
@@ -409,25 +415,30 @@
     piece = leaf_count // NEAR_PIECES if leaf_count % NEAR_PIECES == 0 else leaf_count
     pairs = piece * slot_count * slot_count * 10
 
+    chained = []
+
     def run_piece(number, gate):
         first_leaf = number * piece
         own = target[first_leaf : first_leaf + piece]
         if gate is not None:
             own, unused = lax.optimization_barrier((own, gate))
-        return pl.pallas_call(
-            functools.partial(near_kernel, first_leaf, leaf_count, width),
-            out_shape=jax.ShapeDtypeStruct((piece, 8, slot_count), jnp.float32),
-            in_specs=[pl.BlockSpec(memory_space=pltpu.SMEM)] + [pl.BlockSpec(memory_space=pltpu.VMEM)] * 3,
+        operands = [table, own, source, shift_table] + chained[-1:]
+        result = pl.pallas_call(
+            functools.partial(near_kernel, first_leaf, piece, leaf_count, width),
+            out_shape=jax.ShapeDtypeStruct((leaf_count, 8, slot_count), jnp.float32),
+            in_specs=[pl.BlockSpec(memory_space=pltpu.SMEM)] + [pl.BlockSpec(memory_space=pltpu.VMEM)] * (len(operands) - 1),
             out_specs=pl.BlockSpec(memory_space=pltpu.VMEM),
             scratch_shapes=[pltpu.VMEM((slot_count, 128), jnp.float32)],
+            input_output_aliases={4: 0} if chained else {},
             cost_estimate=pl.CostEstimate(
                 flops=20 * pairs, transcendentals=pairs, bytes_accessed=8 * piece * slot_count * 128
             ),
-        )(table, own, source, shift_table)
+        )(*operands)
+        chained.append(result)
+        return result
 
     def finish_near(outs):
-        out = jnp.concatenate(outs, axis=0)
-        near = jnp.transpose(out[:, :4, :], (1, 0, 2))
+        near = jnp.transpose(chained[-1][:, :4, :], (1, 0, 2))
         return near.reshape(4, size_x, size_y, size_z, slot_count)
 
     return leaf_count // piece, run_piece, finish_near

time: 104 us -> 99 us (0.952)
  waiting for transfers between devices: 11.8 us -> 8.9 us
  local copies, waits for them, and re-layouts: 19.8 us -> 17.1 us
  Pallas kernels: 41.7 us -> 43.2 us
    unnamed x168 -> x151, local copies, waits for them, and re-layouts: 4.99 us -> 1.97 us
    ppermute x5, waiting for transfers between devices: 7.21 us -> 4.32 us  [from_partner(): return lax.ppermute(value, axis, pairs)]
    pallas_call x8, Pallas kernels: 41.7 us -> 43.2 us  [run_piece(): pl.pallas_call(functools.partial(near_kernel, first_leaf, piece, leaf_cou...]
  transfers between devices with their start and end apart: 9 -> 9, of which waited for: 5 -> 3; matrix products, arithmetic and copies ran while one was open for 18% -> 17% of each run, Pallas kernels for 17% -> 16%
where the time goes in v2:
time: 99 us; the launch traced here: 98.7 us
  Pallas kernels  43.2 us (44%)
  local copies, waits for them, and re-layouts  17.1 us (17%)
  other arithmetic  13.2 us (13%)
  starting transfers between devices  10.4 us (11%)
  waiting for transfers between devices  8.9 us (9%)
  matrix products  4.43 us (4%)
  between operations  1.51 us (2%)
    pallas_call x8, Pallas kernels, run_piece(): pl.pallas_call(functools.partial(near_kernel, first_leaf, piece, leaf_cou...  43.2 us
    ppermute x2, starting transfers between devices, extended_joint(): lax.ppermute(jnp.concatenate([piece.reshape(-1) for piece in highs]), axi...  6.1 us
    ppermute x5, waiting for transfers between devices, from_partner(): return lax.ppermute(value, axis, pairs)  4.32 us
    ppermute x2, waiting for transfers between devices, extended_joint(): lax.ppermute(jnp.concatenate([piece.reshape(-1) for piece in lows]), axis...  4.16 us
    ppermute x5, starting transfers between devices, from_partner(): return lax.ppermute(value, axis, pairs)  4.07 us
    dot_general x23, matrix products, matrix_vector(): return jnp.dot(matrix, vector, precision=highest)  3.34 us
    reduce_sum x1, other arithmetic, evaluate(): jnp.sum(cos_local * cosine + sin_local * sine_part, axis=0)  2.97 us
    reduce_sum x1, other arithmetic, leaf_moments(): jnp.sum(cosine * charge[None], axis=-1)  2.91 us
  transfers between devices with their start and end apart: 9, of which 3 were waited for; matrix products, arithmetic and copies ran while one was open for 17% of the time, Pallas kernels for 16%

profile of v2, /device:TPU:0, one launch (start us, length us, event | category | flops | bytes accessed | tf_op | source)
XLA Modules:
  0.0 98.7 jit_solution(7470630983828746279)
XLA Ops:
  0.1 0.8 copy.364
  0.9 0.8 slice.563
  1.7 0.9 add_bitcast_fusion.2
  2.6 0.9 fusion.42
  3.5 2.9 %multiply_reduce_fusion.4 = (f32[40,4,4,2]{0,3,2,1:T(2,128)S(1)}, f32[40,4,4,2]{0,3,2,1:T(2,128)S(1)}) fusion(f32[4,4,2,128]{3,2,1,0:T(2,128)S(1)} %bitcast.458, f32[4,4,2,128]{3,2,1,0:T(2,128)S(1)} %get-tuple-element.75, f32[40]{0:T(128)S(1)} %get-tuple-element.130, f32[4,4,2,128]{3,2,1,0:T(2,128)S(1)} %get-tuple-element.76, f32[40]{0:T(128)S(1)} %get-tuple-element.131, ...), kind=kLoop, calls=%fused_computation.50 | loop fusion | flops 1472000 | bytes 76256 | tf_op jit(solution)/shard_map/reduce_sum | solution.py:111
  8.1 3.9 %collective-permute-start.1 = (f32[5068]{0:T(1024)S(1)}, f32[5068]{0:T(1024)S(1)}, u32[]{:S(2)}, u32[]{:S(2)}) collective-permute-start(f32[5068]{0:T(1024)S(1)} %concatenate.96), channel_id=1, source_target_pairs={{8,0},{16,8},{24,16},{0,24},{9,1},{17,9},{25,17},{1,25},{10,2},{18... | collective-permute-start | bytes 60824 | tf_op jit(solution)/shard_map/ppermute | solution.py:37
  12.8 2.0 %collective-permute-start.4 = (f32[81]{0:T(128)S(1)}, f32[81]{0:T(128)S(1)}, u32[]{:S(2)}, u32[]{:S(2)}) collective-permute-start(f32[81]{0:T(128)S(1)} %bitcast.493), channel_id=1, source_target_pairs={{0,8},{8,0},{16,24},{24,16},{1,9},{9,1},{17,25},{25,17},{2,10},{10... | collective-permute-start | bytes 980 | tf_op jit(solution)/shard_map/ppermute | solution.py:19
  17.4 0.6 copy.369
  18.1 1.4 %fusion.94 = (f32[4,128,4]{2,1,0:T(8,128)}, f32[4,128,4]{2,1,0:T(8,128)}, f32[4,128,4]{2,1,0:T(8,128)}, f32[4,128,4]{2,1,0:T(8,128)}, f32[4,128,4]{2,1,0:T(8,128...) fusion(f32[32,128,4]{2,1,0:T(8,128)S(1)} %bitcast.455), kind=kLoop, calls=%fused_computation.462 | loop fusion | bytes 131072 | tf_op jit(solution)/shard_map/slice | solution.py:422
  22.2 0.7 concatenate.88.refs_0_
  25.3 2.2 %collective-permute-start.3 = (f32[8088]{0:T(1024)S(1)}, f32[8088]{0:T(1024)S(1)}, u32[]{:S(2)}, u32[]{:S(2)}) collective-permute-start(f32[8088]{0:T(1024)S(1)} %concatenate.101), channel_id=1, source_target_pairs={{1,0},{2,1},{3,2},{4,3},{5,4},{6,5},{7,6},{0,7},{9,8},{10,9},{11,1... | collective-permute-start | bytes 97064 | tf_op jit(solution)/shard_map/ppermute | solution.py:37
  28.8 0.4 collective-permute-done.3
  29.6 4.2 %collective-permute-done.2 = f32[8088]{0:T(1024)S(1)} collective-permute-done((f32[8088]{0:T(1024)S(1)}, f32[8088]{0:T(1024)S(1)}, u32[]{:S(2)}, u32[]{:S(2)}) %collective-permute-start.2) | collective-permute-done | bytes 32384 | tf_op jit(solution)/shard_map/ppermute | solution.py:36
  34.4 0.8 pad.11.refs_2_
  35.1 4.4 %shard_map.154.refs_4_ = f32[32,8,128]{2,1,0:T(8,128)} custom-call(s32[1792]{0:T(1024)} %concatenate.88.refs_0_, f32[4,128,4]{2,1,0:T(8,128)} %get-tuple-element.32.refs_1_, f32[73,8,128]{2,1,0:T(8,128)} %pad.11.refs_2_, f32[27,8,128]{2,1,0:T(8,128)} %constant.241.clone.refs_3_), custom_call_target="tpu_custom_call" | custom-call | flops 13107200 | bytes 524288 | tf_op jit(solution)/shard_map/pallas_call | solution.py:426
  39.6 2.0 %collective-permute-start.5 = (f32[81]{0:T(128)S(1)}, f32[81]{0:T(128)S(1)}, u32[]{:S(2)}, u32[]{:S(2)}) collective-permute-start(f32[81]{0:T(128)S(1)} %fusion.12), channel_id=1, source_target_pairs={{0,16},{8,24},{16,0},{24,8},{1,17},{9,25},{17,1},{25,9},{2,18},{10... | collective-permute-start | bytes 980 | tf_op jit(solution)/shard_map/ppermute | solution.py:19
  44.4 0.5 multiply_subtract_fusion.1
  44.9 0.5 maximum_reduce_fusion
  45.4 0.5 multiply_subtract_fusion.2
  45.9 0.5 maximum_reduce_fusion.1
  46.4 4.4 %shard_map.155.refs_4_ = f32[32,8,128]{2,1,0:T(8,128)} custom-call(s32[1792]{0:T(1024)} %concatenate.88.refs_0_, f32[4,128,4]{2,1,0:T(8,128)} %get-tuple-element.14.refs_1_, f32[73,8,128]{2,1,0:T(8,128)} %pad.11.refs_2_, f32[27,8,128]{2,1,0:T(8,128)} %constant.241.clone.refs_3_, f32[32,8,128]{2,1,0:T(8,128)} %shard_map.154.refs_4_), custom_call_target="tpu_custom_call", output_to_operand_aliasing={{}: (4, {})} | custom-call | flops 13107200 | bytes 524288 | tf_op jit(solution)/shard_map/pallas_call | solution.py:426
  51.1 5.8 %shard_map.156.refs_4_ = f32[32,8,128]{2,1,0:T(8,128)} custom-call(s32[1792]{0:T(1024)} %concatenate.88.refs_0_, f32[4,128,4]{2,1,0:T(8,128)} %get-tuple-element.16.refs_1_, f32[73,8,128]{2,1,0:T(8,128)} %pad.11.refs_2_, f32[27,8,128]{2,1,0:T(8,128)} %constant.241.clone.refs_3_, f32[32,8,128]{2,1,0:T(8,128)} %shard_map.155.refs_4_), custom_call_target="tpu_custom_call", output_to_operand_aliasing={{}: (4, {})} | custom-call | flops 13107200 | bytes 524288 | tf_op jit(solution)/shard_map/pallas_call | solution.py:426
  57.2 5.1 %shard_map.157.refs_4_ = f32[32,8,128]{2,1,0:T(8,128)} custom-call(s32[1792]{0:T(1024)} %concatenate.88.refs_0_, f32[4,128,4]{2,1,0:T(8,128)} %get-tuple-element.19.refs_1_, f32[73,8,128]{2,1,0:T(8,128)} %pad.11.refs_2_, f32[27,8,128]{2,1,0:T(8,128)} %constant.241.clone.refs_3_, f32[32,8,128]{2,1,0:T(8,128)} %shard_map.156.refs_4_), custom_call_target="tpu_custom_call", output_to_operand_aliasing={{}: (4, {})} | custom-call | flops 13107200 | bytes 524288 | tf_op jit(solution)/shard_map/pallas_call | solution.py:426
  62.5 5.4 %shard_map.158.refs_4_ = f32[32,8,128]{2,1,0:T(8,128)} custom-call(s32[1792]{0:T(1024)} %concatenate.88.refs_0_, f32[4,128,4]{2,1,0:T(8,128)} %get-tuple-element.18.refs_1_, f32[73,8,128]{2,1,0:T(8,128)} %pad.11.refs_2_, f32[27,8,128]{2,1,0:T(8,128)} %constant.241.clone.refs_3_, f32[32,8,128]{2,1,0:T(8,128)} %shard_map.157.refs_4_), custom_call_target="tpu_custom_call", output_to_operand_aliasing={{}: (4, {})} | custom-call | flops 13107200 | bytes 524288 | tf_op jit(solution)/shard_map/pallas_call | solution.py:426
  67.9 6.6 %shard_map.159.refs_4_ = f32[32,8,128]{2,1,0:T(8,128)} custom-call(s32[1792]{0:T(1024)} %concatenate.88.refs_0_, f32[4,128,4]{2,1,0:T(8,128)} %get-tuple-element.34.refs_1_, f32[73,8,128]{2,1,0:T(8,128)} %pad.11.refs_2_, f32[27,8,128]{2,1,0:T(8,128)} %constant.241.clone.refs_3_, f32[32,8,128]{2,1,0:T(8,128)} %shard_map.158.refs_4_), custom_call_target="tpu_custom_call", output_to_operand_aliasing={{}: (4, {})} | custom-call | flops 13107200 | bytes 524288 | tf_op jit(solution)/shard_map/pallas_call | solution.py:426
  74.5 5.7 %shard_map.160.refs_4_ = f32[32,8,128]{2,1,0:T(8,128)} custom-call(s32[1792]{0:T(1024)} %concatenate.88.refs_0_, f32[4,128,4]{2,1,0:T(8,128)} %get-tuple-element.35.refs_1_, f32[73,8,128]{2,1,0:T(8,128)} %pad.11.refs_2_, f32[27,8,128]{2,1,0:T(8,128)} %constant.241.clone.refs_3_, f32[32,8,128]{2,1,0:T(8,128)} %shard_map.159.refs_4_), custom_call_target="tpu_custom_call", output_to_operand_aliasing={{}: (4, {})} | custom-call | flops 13107200 | bytes 524288 | tf_op jit(solution)/shard_map/pallas_call | solution.py:426
  80.2 5.7 %shard_map.161 = f32[32,8,128]{2,1,0:T(8,128)} custom-call(s32[1792]{0:T(1024)} %concatenate.88.refs_0_, f32[4,128,4]{2,1,0:T(8,128)} %get-tuple-element.36.refs_1_, f32[73,8,128]{2,1,0:T(8,128)} %pad.11.refs_2_, f32[27,8,128]{2,1,0:T(8,128)} %constant.241.clone.refs_3_, f32[32,8,128]{2,1,0:T(8,128)} %shard_map.160.refs_4_), custom_call_target="tpu_custom_call", output_to_operand_aliasing={{}: (4, {})} | custom-call | flops 13107200 | bytes 524288 | tf_op jit(solution)/shard_map/pallas_call | solution.py:426
  85.9 0.9 slice_bitcast_fusion
  87.1 4.3 %collective-permute-done.8 = f32[81]{0:T(128)S(1)} collective-permute-done((f32[81]{0:T(128)S(1)}, f32[81]{0:T(128)S(1)}, u32[]{:S(2)}, u32[]{:S(2)}) %collective-permute-start.8) | collective-permute-done | bytes 356 | tf_op jit(solution)/shard_map/ppermute | solution.py:19
  93.9 0.5 convolution_bitcast_fusion.1
  94.9 3.0 %add_reduce_fusion = (f32[4,4,2,128]{3,2,1,0:T(2,128)S(1)}, f32[4,4,2,128]{3,2,1,0:T(2,128)S(1)}, f32[4,4,2,128]{3,2,1,0:T(2,128)S(1)}, f32[4,4,2,128]{3,2,1,0:T(2,128)S(1)}) fusion(f32[40,4,4,2]{0,3,2,1:T(2,128)S(1)} %copy.456, f32[40,4,4,2]{0,3,2,1:T(2,128)S(1)} %copy.455, f32[4,4,2,128]{3,2,1,0:T(2,128)S(1)} %get-tuple-element.75, ...), kind=kLoop, calls=%fused_computation.48 | loop fusion | flops 2932736 | bytes 125408 | tf_op jit(solution)/shard_map/reduce_sum | solution.py:123
  98.0 0.7 pad_maximum_fusion.1
  (346 shorter events, 18.2 us)
Async XLA Ops:
  0.0 6.7 %copy-start = (bf16[8,81,81]{2,0,1:T(8,128)(2,1)S(1)}, bf16[8,81,81]{2,0,1:T(8,128)(2,1)}, u32[]{:S(2)}) copy-start(bf16[8,81,81]{2,0,1:T(8,128)(2,1)} %param.19) | copy-start | bytes 314932
  0.0 12.7 %copy-start.6 = (bf16[81,81]{1,0:T(8,128)(2,1)S(1)}, bf16[81,81]{1,0:T(8,128)(2,1)}, u32[]{:S(2)}) copy-start(bf16[81,81]{1,0:T(8,128)(2,1)} %param.23) | copy-start | bytes 39370
  0.0 14.9 %copy-start.5 = (s32[26,4,4,2]{0,3,2,1:T(2,128)S(1)}, s32[26,4,4,2]{0,3,2,1:T(2,128)}, u32[]{:S(2)}) copy-start(s32[26,4,4,2]{0,3,2,1:T(2,128)} %param.18) | copy-start | bytes 9988
  8.1 14.8 %collective-permute-start.1 = (f32[5068]{0:T(1024)S(1)}, f32[5068]{0:T(1024)S(1)}, u32[]{:S(2)}, u32[]{:S(2)}) collective-permute-start(f32[5068]{0:T(1024)S(1)} %concatenate.96), channel_id=1, source_target_pairs={{8,0},{16,8},{24,16},{0,24},{9,1},{17,9},{25,17},{1,25},{10,2},{18... | collective-permute-start | bytes 60824 | tf_op jit(solution)/shard_map/ppermute | solution.py:37
  12.4 10.8 %collective-permute-start = (f32[5068]{0:T(1024)S(1)}, f32[5068]{0:T(1024)S(1)}, u32[]{:S(2)}, u32[]{:S(2)}) collective-permute-start(f32[5068]{0:T(1024)S(1)} %concatenate.95), channel_id=1, source_target_pairs={{0,8},{8,16},{16,24},{24,0},{1,9},{9,17},{17,25},{25,1},{2,10},{10... | collective-permute-start | bytes 60824 | tf_op jit(solution)/shard_map/ppermute | solution.py:36
  12.8 14.7 %collective-permute-start.4 = (f32[81]{0:T(128)S(1)}, f32[81]{0:T(128)S(1)}, u32[]{:S(2)}, u32[]{:S(2)}) collective-permute-start(f32[81]{0:T(128)S(1)} %bitcast.493), channel_id=1, source_target_pairs={{0,8},{8,0},{16,24},{24,16},{1,9},{9,1},{17,25},{25,17},{2,10},{10... | collective-permute-start | bytes 980 | tf_op jit(solution)/shard_map/ppermute | solution.py:19
  18.0 1.5 %copy-start.2 = (bf16[2,2,81,81]{3,1,2,0:T(2,128)(2,1)S(1)}, bf16[2,2,81,81]{3,1,2,0:T(2,128)(2,1)}, u32[]{:S(2)}) copy-start(bf16[2,2,81,81]{3,1,2,0:T(2,128)(2,1)} %param.25) | copy-start | bytes 157468
  18.0 1.9 %copy-start.3 = (bf16[2,2,81,81]{3,1,2,0:T(2,128)(2,1)S(1)}, bf16[2,2,81,81]{3,1,2,0:T(2,128)(2,1)}, u32[]{:S(2)}) copy-start(bf16[2,2,81,81]{3,1,2,0:T(2,128)(2,1)} %param.26) | copy-start | bytes 157468
  18.1 2.0 %copy-start.4 = (bf16[2,2,81,81]{3,1,2,0:T(2,128)(2,1)S(1)}, bf16[2,2,81,81]{3,1,2,0:T(2,128)(2,1)}, u32[]{:S(2)}) copy-start(bf16[2,2,81,81]{3,1,2,0:T(2,128)(2,1)} %param.27) | copy-start | bytes 157468
  18.1 2.6 %copy-start.14 = (f32[26]{0:T(128)S(1)}, f32[26]{0:T(128)}, u32[]{:S(2)}) copy-start(f32[26]{0:T(128)} %constant.264) | copy-start | bytes 316
  18.1 2.6 %copy-start.15 = (f32[26]{0:T(128)S(1)}, f32[26]{0:T(128)}, u32[]{:S(2)}) copy-start(f32[26]{0:T(128)} %constant.262) | copy-start | bytes 316
  18.1 2.6 %copy-start.16 = (f32[26]{0:T(128)S(1)}, f32[26]{0:T(128)}, u32[]{:S(2)}) copy-start(f32[26]{0:T(128)} %constant.260) | copy-start | bytes 316
  18.1 2.8 %copy-start.11 = (f32[98]{0:T(128)S(1)}, f32[98]{0:T(128)}, u32[]{:S(2)}) copy-start(f32[98]{0:T(128)} %constant.258) | copy-start | bytes 1180
  18.1 2.8 %copy-start.12 = (f32[98]{0:T(128)S(1)}, f32[98]{0:T(128)}, u32[]{:S(2)}) copy-start(f32[98]{0:T(128)} %constant.256) | copy-start | bytes 1180
  18.1 2.8 %copy-start.13 = (f32[98]{0:T(128)S(1)}, f32[98]{0:T(128)}, u32[]{:S(2)}) copy-start(f32[98]{0:T(128)} %constant.254) | copy-start | bytes 1180
  25.3 4.0 %collective-permute-start.3 = (f32[8088]{0:T(1024)S(1)}, f32[8088]{0:T(1024)S(1)}, u32[]{:S(2)}, u32[]{:S(2)}) collective-permute-start(f32[8088]{0:T(1024)S(1)} %concatenate.101), channel_id=1, source_target_pairs={{1,0},{2,1},{3,2},{4,3},{5,4},{6,5},{7,6},{0,7},{9,8},{10,9},{11,1... | collective-permute-start | bytes 97064 | tf_op jit(solution)/shard_map/ppermute | solution.py:37
  28.5 5.3 %collective-permute-start.2 = (f32[8088]{0:T(1024)S(1)}, f32[8088]{0:T(1024)S(1)}, u32[]{:S(2)}, u32[]{:S(2)}) collective-permute-start(f32[8088]{0:T(1024)S(1)} %concatenate.100), channel_id=1, source_target_pairs={{0,1},{1,2},{2,3},{3,4},{4,5},{5,6},{6,7},{7,0},{8,9},{9,10},{10,1... | collective-permute-start | bytes 97064 | tf_op jit(solution)/shard_map/ppermute | solution.py:36
  39.6 11.2 %collective-permute-start.5 = (f32[81]{0:T(128)S(1)}, f32[81]{0:T(128)S(1)}, u32[]{:S(2)}, u32[]{:S(2)}) collective-permute-start(f32[81]{0:T(128)S(1)} %fusion.12), channel_id=1, source_target_pairs={{0,16},{8,24},{16,0},{24,8},{1,17},{9,25},{17,1},{25,9},{2,18},{10... | collective-permute-start | bytes 980 | tf_op jit(solution)/shard_map/ppermute | solution.py:19
  50.9 6.0 %collective-permute-start.6 = (f32[81]{0:T(128)S(1)}, f32[81]{0:T(128)S(1)}, u32[]{:S(2)}, u32[]{:S(2)}) collective-permute-start(f32[81]{0:T(128)S(1)} %fusion.11), channel_id=1, source_target_pairs={{0,1},{1,0},{2,3},{3,2},{4,5},{5,4},{6,7},{7,6},{8,9},{9,8},{10,11... | collective-permute-start | bytes 980 | tf_op jit(solution)/shard_map/ppermute | solution.py:19
  57.0 5.3 %collective-permute-start.7 = (f32[81]{0:T(128)S(1)}, f32[81]{0:T(128)S(1)}, u32[]{:S(2)}, u32[]{:S(2)}) collective-permute-start(f32[81]{0:T(128)S(1)} %fusion.10), channel_id=1, source_target_pairs={{0,2},{1,3},{2,0},{3,1},{4,6},{5,7},{6,4},{7,5},{8,10},{9,11},{10,... | collective-permute-start | bytes 980 | tf_op jit(solution)/shard_map/ppermute | solution.py:19
  67.9 23.6 %copy-start.7 = (bf16[81,81]{1,0:T(8,128)(2,1)S(1)}, bf16[81,81]{1,0:T(8,128)(2,1)}, u32[]{:S(2)}) copy-start(bf16[81,81]{1,0:T(8,128)(2,1)} %param.28) | copy-start | bytes 39370
  67.9 25.5 %copy-start.8 = (bf16[81,81]{1,0:T(8,128)(2,1)S(1)}, bf16[81,81]{1,0:T(8,128)(2,1)}, u32[]{:S(2)}) copy-start(bf16[81,81]{1,0:T(8,128)(2,1)} %param.24) | copy-start | bytes 39370
  67.9 25.9 %copy-start.9 = (bf16[81,81]{1,0:T(8,128)(2,1)S(1)}, bf16[81,81]{1,0:T(8,128)(2,1)}, u32[]{:S(2)}) copy-start(bf16[81,81]{1,0:T(8,128)(2,1)} %param.22) | copy-start | bytes 39370
  67.9 26.0 %copy-start.1 = (bf16[8,81,81]{2,0,1:T(8,128)(2,1)S(1)}, bf16[8,81,81]{2,0,1:T(8,128)(2,1)}, u32[]{:S(2)}) copy-start(bf16[8,81,81]{2,0,1:T(8,128)(2,1)} %param.20) | copy-start | bytes 314932
  67.9 26.5 %copy-start.10 = (bf16[81,81]{1,0:T(8,128)(2,1)S(1)}, bf16[81,81]{1,0:T(8,128)(2,1)}, u32[]{:S(2)}) copy-start(bf16[81,81]{1,0:T(8,128)(2,1)} %param.21) | copy-start | bytes 39370
  86.9 4.5 %collective-permute-start.8 = (f32[81]{0:T(128)S(1)}, f32[81]{0:T(128)S(1)}, u32[]{:S(2)}, u32[]{:S(2)}) collective-permute-start(f32[81]{0:T(128)S(1)} %fusion.9), channel_id=1, source_target_pairs={{0,4},{1,5},{2,6},{3,7},{4,0},{5,1},{6,2},{7,3},{8,12},{9,13},{10,... | collective-permute-start | bytes 980 | tf_op jit(solution)/shard_map/ppermute | solution.py:19
